TPU v7x, 256 devices: a whole 4x4x8 slice. The times are simulated.
256 devices in a mesh: pts: 128 (over y, z, x), rep: 2 (over core).
Axes of the slice: x: 4, y: 4, z: 8, core: 2. Of those that a mesh axis runs over, the one named last changes fastest.
Arguments:
- src_points: bfloat16 [393216, 256], P('pts'), may hold values from -7 to 7
- tgt_points: bfloat16 [393216, 256], P('pts'), may hold values from -7 to 7
- pair_source: int32 [24576], P(('pts', 'rep')), may hold values from -1 to 3071, as said below
- pair_target: int32 [24576], P(('pts', 'rep')), may hold values from -1 to 3071, as said below
- pair_count: int32 [256], P(('pts', 'rep')), may hold values from 12 to 96, as said below
Outputs:
- source_dual: float32 [393216], P('pts')
- target_dual: float32 [393216], P('pts')
- target_grad: float32 [393216, 256], P('pts')
Inputs may be any that keep to these rules, and one draw needn't show every extreme that they name: `pair_source`: for the device at index d of pts+rep (pts index p = d // 2, rep index r = d % 2), the first pair_count[d] of its 96 slots name source blocks p * 24 to (p + 1) * 24 - 1; its other slots hold -1. `pair_target`: A listed target block t has owner t // 24; one device's listed slots name different owners, and only blocks whose index t % 24 lies in r * 12 to (r + 1) * 12 - 1; unlisted slots hold -1. No pair of blocks is listed twice; every source block and every target block is listed somewhere; some owner is named by every device. `pair_count`: some device lists 96 pairs.
All inputs are finite; a program needn't handle non-finite values.
Results may differ from a plain program's by a relative error of at most 0.0016.
Values may be sent and summed in bfloat16 or wider, within the bound.
No kernel may reach another device: no remote copies, remote signals or barrier semaphores. Data moves between devices by JAX's collectives and lax.ppermute only.
A program may use at most 192 MiB of HBM per device.

v0:
```python
import jax
import jax.numpy as jnp
from jax import lax
from jax.experimental import pallas as pl
from jax.experimental.pallas import tpu as pltpu
from jax.sharding import PartitionSpec as P

BLOCK = 128
ITERS = 3


EPSILON = 0.05
NEG_BIG = -1e30
INV_EPS = 1.0 / EPSILON
SWEEP_STEP = 64
GRADIENT_STEP = 32


def columns_of(duals, step):
    pairs, side = duals.shape
    shaped = duals.reshape(pairs // step, step, side).transpose(0, 2, 1)
    return jnp.pad(shaped, ((0, 0), (0, 0), (0, side - step)))


def sweep_kernel(grid_ref, dual_ref, out_ref):
    side = grid_ref.shape[1]
    dual_cols = dual_ref[0]
    for p in range(grid_ref.shape[0]):
        dual_col = jnp.broadcast_to(dual_cols[:, p : p + 1], (side, side))
        scores = (dual_col - grid_ref[p]) * INV_EPS
        peak = jnp.max(scores, axis=0, keepdims=True)
        mass = jnp.sum(jnp.exp(scores - peak), axis=0, keepdims=True)
        out_ref[p : p + 1, :] = peak + jnp.log(mass)


def sweep(grids, duals):
    pairs, side, _ = grids.shape
    return pl.pallas_call(
        sweep_kernel,
        grid=(pairs // SWEEP_STEP,),
        in_specs=[
            pl.BlockSpec((SWEEP_STEP, side, side), lambda s: (s, 0, 0)),
            pl.BlockSpec((1, side, side), lambda s: (s, 0, 0)),
        ],
        out_specs=pl.BlockSpec((SWEEP_STEP, side), lambda s: (s, 0)),
        out_shape=jax.ShapeDtypeStruct((pairs, side), jnp.float32),
        cost_estimate=pl.CostEstimate(
            flops=8 * pairs * side * side,
            transcendentals=pairs * side * side,
            bytes_accessed=4 * pairs * side * (side + 2),
        ),
    )(grids, columns_of(duals, SWEEP_STEP))


def gradient_kernel(
    keys_ref, grid_t_ref, source_ref, target_ref, rows_ref, half_ref, out_ref, mass_ref
):
    step = pl.program_id(0)
    side = grid_t_ref.shape[1]

    @pl.when(step == 0)
    def _():
        out_ref[...] = jnp.zeros_like(out_ref)
        mass_ref[...] = jnp.zeros_like(mass_ref)

    target_cols = target_ref[0]
    ones = jnp.ones((side, side), jnp.bfloat16)
    for p in range(grid_t_ref.shape[0]):
        key = keys_ref[step * GRADIENT_STEP + p]
        slot = jnp.maximum(key, 0)
        target_col = jnp.broadcast_to(target_cols[:, p : p + 1], (side, side))
        plan_t = jnp.exp((source_ref[p : p + 1, :] + target_col - grid_t_ref[p]) * INV_EPS)
        plan_t = jnp.where(key >= 0, plan_t, 0.0)
        weights = plan_t.astype(jnp.bfloat16)
        remainder = (plan_t - weights.astype(jnp.float32)).astype(jnp.bfloat16)
        mass = jnp.dot(weights, ones, preferred_element_type=jnp.float32) + jnp.dot(
            remainder, ones, preferred_element_type=jnp.float32
        )
        numerator = jnp.dot(weights, rows_ref[p], preferred_element_type=jnp.float32)
        out_ref[slot] -= numerator
        mass_ref[slot] += mass

    @pl.when(step == pl.num_programs(0) - 1)
    def _():
        mass = mass_ref[...]
        out_ref[...] += half_ref[...].astype(jnp.float32) * jnp.concatenate([mass, mass], axis=2)


def gradient_sums(keys, grids_t, source_duals, target_duals, rows, half_targets):
    pairs, side, _ = grids_t.shape
    width = rows.shape[2]
    half = half_targets.shape[0]
    return pl.pallas_call(
        gradient_kernel,
        grid_spec=pltpu.PrefetchScalarGridSpec(
            num_scalar_prefetch=1,
            grid=(pairs // GRADIENT_STEP,),
            in_specs=[
                pl.BlockSpec((GRADIENT_STEP, side, side), lambda s, k: (s, 0, 0)),
                pl.BlockSpec((GRADIENT_STEP, side), lambda s, k: (s, 0)),
                pl.BlockSpec((1, side, side), lambda s, k: (s, 0, 0)),
                pl.BlockSpec((GRADIENT_STEP, side, width), lambda s, k: (s, 0, 0)),
                pl.BlockSpec((half, side, width), lambda s, k: (0, 0, 0)),
            ],
            out_specs=pl.BlockSpec((half, side, width), lambda s, k: (0, 0, 0)),
            scratch_shapes=[pltpu.VMEM((half, side, side), jnp.float32)],
        ),
        out_shape=jax.ShapeDtypeStruct((half, side, width), jnp.float32),
        compiler_params=pltpu.CompilerParams(dimension_semantics=("arbitrary",)),
        cost_estimate=pl.CostEstimate(
            flops=2 * pairs * side * side * width + 8 * pairs * side * side,
            transcendentals=pairs * side * side,
            bytes_accessed=pairs * side * (4 * side + 2 * width) + half * side * width * 6,
        ),
    )(keys, grids_t, source_duals, columns_of(target_duals, GRADIENT_STEP), rows, half_targets)


def both_halves(mine, rep_index):
    other = lax.ppermute(mine, "rep", [(0, 1), (1, 0)])
    return jnp.where(
        rep_index == 0,
        jnp.concatenate([mine, other], axis=0),
        jnp.concatenate([other, mine], axis=0),
    )


def squares(blocks_in):
    return jnp.sum(jnp.square(blocks_in.astype(jnp.float32)), axis=-1)


def pair_costs(source_rows, target_rows, source_sq, target_sq):
    inner_dot = jnp.einsum(
        "gid,gjd->gij", source_rows, target_rows, preferred_element_type=jnp.float32
    )
    inner_dot_t = jnp.einsum(
        "gjd,gid->gji", target_rows, source_rows, preferred_element_type=jnp.float32
    )
    width = source_rows.shape[2]
    grid = (source_sq[:, :, None] + target_sq[:, None, :] - 2.0 * inner_dot) / width
    grid_t = (source_sq[:, None, :] + target_sq[:, :, None] - 2.0 * inner_dot_t) / width
    return grid, grid_t


def pair_lse(scores, axis):
    peaks = jnp.max(scores, axis=axis)
    masses = jnp.sum(jnp.exp(scores - jnp.expand_dims(peaks, axis)), axis=axis)
    return peaks + jnp.log(masses)


def combine_by(values, block_key, key_count):
    member = (block_key[:, None] == jnp.arange(key_count)[None, :])[:, :, None]
    maxima = jnp.max(jnp.where(member, values[:, None, :], NEG_BIG), axis=0)
    shifts = jnp.where(member, values[:, None, :] - maxima[None, :, :], NEG_BIG)
    totals = jnp.sum(jnp.where(member, jnp.exp(shifts), 0.0), axis=0)
    return maxima, totals


def swap_rep(value):
    return lax.ppermute(value, "rep", [(0, 1), (1, 0)])


def a2a(value):
    return lax.all_to_all(value, "pts", split_axis=0, concat_axis=0, tiled=True)


def on_device(src_points, tgt_points, pair_source, pair_target, pair_count):
    peer_count = lax.axis_size("pts")
    point_rows, feat_width = src_points.shape
    block_len = BLOCK
    blocks = point_rows // block_len
    half_blocks = blocks // lax.axis_size("rep")
    rep_index = lax.axis_index("rep")
    lower_block = rep_index * half_blocks
    own_sources = src_points.reshape(blocks, block_len, feat_width)
    own_targets = tgt_points.reshape(blocks, block_len, feat_width)

    pair_total = pair_count[0]
    slot_total = pair_source.shape[0]
    usable = jnp.arange(slot_total) < pair_total
    source_local = jnp.where(usable, pair_source % blocks, 0)
    owner_ids = jnp.where(usable, pair_target // blocks, 0)
    target_local = jnp.where(usable, pair_target % blocks, 0)
    matched = (owner_ids[:, None] == jnp.arange(peer_count)[None, :]) & usable[:, None]
    wanted = jnp.max(jnp.where(matched, target_local[:, None], -1), axis=0)
    source_of_owner = jnp.max(jnp.where(matched, source_local[:, None], -1), axis=0)
    served = source_of_owner >= 0
    source_index = jnp.maximum(source_of_owner, 0)
    outgoing = own_sources[source_index]
    asked_info = jnp.stack(
        [
            squares(own_sources)[source_index],
            jnp.broadcast_to(wanted.astype(jnp.float32)[:, None], (peer_count, block_len)),
        ],
        axis=1,
    )
    asked_info = a2a(asked_info)
    received = a2a(outgoing)
    asked_ids = asked_info[:, 1, 0].astype(jnp.int32)
    received_sq = asked_info[:, 0, :]

    valid = asked_ids >= 0
    half_key = jnp.where(valid, asked_ids - lower_block, -1)
    half_pick = jnp.clip(half_key, 0, half_blocks - 1)
    own_half = lax.dynamic_slice_in_dim(own_targets, lower_block, half_blocks, 0)
    pair_targets = own_half[half_pick]
    target_sq = squares(own_half)[half_pick]
    cost_grid, cost_grid_t = pair_costs(received, pair_targets, received_sq, target_sq)

    target_half = jnp.zeros((half_blocks, block_len), jnp.float32)
    for round_no in range(ITERS):
        target_here = target_half[half_pick]
        row_lse = sweep(cost_grid_t, target_here)
        row_back = a2a(row_lse)
        maxima, totals = combine_by(row_back, source_of_owner, blocks)
        other_maxima, other_totals = swap_rep((maxima, totals))
        merged = jnp.maximum(maxima, other_maxima)
        merged_totals = totals * jnp.exp(maxima - merged) + other_totals * jnp.exp(
            other_maxima - merged
        )
        source_dual = -EPSILON * (merged + jnp.log(merged_totals))
        sent_duals = jnp.where(served[:, None], source_dual[source_index], 0.0)
        source_here = a2a(sent_duals)
        column_lse = sweep(cost_grid, source_here)
        col_max, col_tot = combine_by(column_lse, half_key, half_blocks)
        target_half = -EPSILON * (col_max + jnp.log(col_tot))

    target_here = target_half[half_pick]
    gradient_half = gradient_sums(
        half_key, cost_grid_t, source_here, target_here, received, own_half
    )
    target_dual = both_halves(target_half, rep_index)
    gradient = both_halves(gradient_half, rep_index)
    return (
        source_dual.reshape(-1),
        target_dual.reshape(-1),
        gradient.reshape(blocks * block_len, feat_width),
    )


def solution(mesh):
    return jax.shard_map(
        on_device,
        mesh=mesh,
        in_specs=(
            P("pts", None),
            P("pts", None),
            P(("pts", "rep")),
            P(("pts", "rep")),
            P(("pts", "rep")),
        ),
        out_specs=(P("pts"), P("pts"), P("pts", None)),
        check_vma=False,
    )
```

profile of v0, /device:TPU:1, one launch (start us, length us, event | category | flops | bytes accessed | tf_op | source)
XLA Modules:
  0.0 429.8 jit_solution(15225280167710827567)
XLA Ops:
  1.4 0.7 fusion.9
  2.3 1.9 multiply_reduce_fusion
  4.2 0.6 gather_fusion
  4.9 0.8 copy.43
  5.7 16.3 %all-to-all-start = ((f32[128,2,128]{2,1,0:T(2,128)}), f32[128,2,128]{2,1,0:T(2,128)S(1)}, u32[]{:S(2)}, u32[]{:S(2)}) async-start(f32[128,2,128]{2,1,0:T(2,128)} %copy.43), calls=%async_computation | async-start | bytes 262144 | tf_op jit(solution)/shard_map/all_to_all | solution.py:163
  22.0 6.3 %gather_fusion.3 = bf16[128,128,256]{2,1,0:T(8,128)(2,1)} fusion(bf16[24,128,256]{2,1,0:T(8,128)(2,1)S(1)} %bitcast.56, s32[1024]{0:T(1024)S(1)} %pad_clamp_fusion.1), kind=kCustom, calls=%fused_computation.3 | custom fusion | bytes 16777728 | tf_op jit(solution)/shard_map/gather | solution.py:188
  28.3 4.6 %all-to-all-done = f32[128,2,128]{2,1,0:T(2,128)S(1)} async-done(((f32[128,2,128]{2,1,0:T(2,128)}), f32[128,2,128]{2,1,0:T(2,128)S(1)}, u32[]{:S(2)}, u32[]{:S(2)}) %all-to-all-start) | async-done | bytes 131104 | tf_op jit(solution)/shard_map/all_to_all | solution.py:163
  33.0 9.5 %all-to-all-start.1 = ((bf16[128,128,256]{2,1,0:T(8,128)(2,1)}), bf16[128,128,256]{2,1,0:T(8,128)(2,1)}, u32[]{:S(2)}, u32[]{:S(2)}) async-start(bf16[128,128,256]{2,1,0:T(8,128)(2,1)} %gather_fusion.3), calls=%async_computation.1 | async-start | bytes 16777216 | tf_op jit(solution)/shard_map/all_to_all | solution.py:163
  42.9 4.7 %fusion.12 = (s32[128]{0:T(128)S(1)}, s32[128]{0:T(128)S(1)}) fusion(s32[]{:T(128)S(6)} %mul.45, f32[128,2,128]{2,1,0:T(2,128)S(1)} %all-to-all-done), kind=kLoop, calls=%fused_computation.72 | loop fusion | flops 640 | bytes 1540 | tf_op jit(solution)/shard_map/jit(_where)/select_n | solution.py:202
  47.6 0.6 gather_fusion.1
  48.2 6.4 %gather_fusion.2 = bf16[128,128,256]{2,1,0:T(8,128)(2,1)} fusion(bf16[12,128,256]{2,1,0:T(8,128)(2,1)S(1)} %get-tuple-element.8.half_ref, s32[1024]{0:T(1024)S(1)} %pad_clamp_fusion), kind=kCustom, calls=%fused_computation.2 | custom fusion | bytes 16777728 | tf_op jit(solution)/shard_map/gather | solution.py:205
  54.6 0.6 gather_fusion.4
  55.3 0.7 pad.23.dual_ref
  56.0 168.5 %all-to-all-done.1.rows_ref = bf16[128,128,256]{2,1,0:T(8,128)(2,1)} async-done(((bf16[128,128,256]{2,1,0:T(8,128)(2,1)}), bf16[128,128,256]{2,1,0:T(8,128)(2,1)}, u32[]{:S(2)}, u32[]{:S(2)}) %all-to-all-start.1) | async-done | bytes 8388640 | tf_op jit(solution)/shard_map/all_to_all | solution.py:163
  224.5 9.3 %subtract_multiply_fusion.1.grid_ref.grid_t_ref = f32[128,128,128]{2,1,0:T(8,128)} fusion(f32[128,128]{1,0:T(8,128)S(1)} %gather_fusion.1, f32[128,128]{1,0:T(8,128)S(1)} %bitcast.60, bf16[128,128,256]{2,1,0:T(8,128)(2,1)} %gather_fusion.2, bf16[128,128,256]{2,1,0:T(8,128)(2,1)} %all-to-all-done.1.rows_ref), kind=kOutput, calls=%fused_computation.12 | convolution fusion | flops 1082130432 | bytes 25296896 | tf_op jit(solution)/shard_map/gjd,gid->gji/dot_general | solution.py:135
  233.8 5.4 %shard_map.76 = f32[128,128]{1,0:T(8,128)} custom-call(f32[128,128,128]{2,1,0:T(8,128)} %subtract_multiply_fusion.1.grid_ref.grid_t_ref, f32[2,128,128]{2,1,0:T(8,128)} %pad.23.dual_ref), custom_call_target="tpu_custom_call" | custom-call | flops 16777216 | bytes 8519680 | tf_op jit(solution)/shard_map/pallas_call | solution.py:38
  239.3 10.5 %all-to-all-start.2 = ((f32[128,1,128]{2,1,0:T(1,128)}), f32[128,1,128]{2,1,0:T(1,128)S(1)}, u32[]{:S(2)}, u32[]{:S(2)}) async-start(f32[128,1,128]{2,1,0:T(1,128)} %bitcast.72), calls=%async_computation.2 | async-start | bytes 131072 | tf_op jit(solution)/shard_map/all_to_all | solution.py:163
  249.8 10.6 %all-to-all-done.2 = f32[128,1,128]{2,1,0:T(1,128)S(1)} async-done(((f32[128,1,128]{2,1,0:T(1,128)}), f32[128,1,128]{2,1,0:T(1,128)S(1)}, u32[]{:S(2)}, u32[]{:S(2)}) %all-to-all-start.2) | async-done | bytes 65568 | tf_op jit(solution)/shard_map/all_to_all | solution.py:163
  260.4 0.6 select_reduce_fusion.5
  260.9 0.6 select_reduce_fusion.4
  261.5 3.6 collective-permute-start
  265.2 1.1 collective-permute-done.1
  266.3 0.6 gather_fusion.5
  267.0 0.7 bitcast_select_fusion.2
  267.7 6.4 %all-to-all-start.3 = ((f32[128,1,128]{2,1,0:T(1,128)}), f32[128,1,128]{2,1,0:T(1,128)S(1)}, u32[]{:S(2)}, u32[]{:S(2)}) async-start(f32[128,1,128]{2,1,0:T(1,128)} %bitcast.13), calls=%async_computation.3 | async-start | bytes 131072 | tf_op jit(solution)/shard_map/all_to_all | solution.py:163
  274.0 9.3 %subtract_multiply_fusion.grid_ref = f32[128,128,128]{2,1,0:T(8,128)} fusion(f32[128,128]{1,0:T(8,128)S(1)} %gather_fusion.1, f32[128,128]{1,0:T(8,128)S(1)} %bitcast.61, bf16[128,128,256]{2,1,0:T(8,128)(2,1)} %all-to-all-done.1.rows_ref, bf16[128,128,256]{2,1,0:T(8,128)(2,1)} %gather_fusion.2), kind=kOutput, calls=%fused_computation.11 | convolution fusion | flops 1082130432 | bytes 25296896 | tf_op jit(solution)/shard_map/gid,gjd->gij/dot_general | solution.py:132
  283.3 1.3 all-to-all-done.3
  284.8 0.7 pad.24.dual_ref
  285.4 5.4 %shard_map.77 = f32[128,128]{1,0:T(8,128)} custom-call(f32[128,128,128]{2,1,0:T(8,128)} %subtract_multiply_fusion.grid_ref, f32[2,128,128]{2,1,0:T(8,128)} %pad.24.dual_ref), custom_call_target="tpu_custom_call" | custom-call | flops 16777216 | bytes 8519680 | tf_op jit(solution)/shard_map/pallas_call | solution.py:38
  290.8 1.1 select_reduce_fusion.11
  292.0 1.1 select_reduce_fusion.10
  293.1 0.6 gather_fusion.6
  293.9 0.7 pad.25.dual_ref
  294.5 5.4 %shard_map.78 = f32[128,128]{1,0:T(8,128)} custom-call(f32[128,128,128]{2,1,0:T(8,128)} %subtract_multiply_fusion.1.grid_ref.grid_t_ref, f32[2,128,128]{2,1,0:T(8,128)} %pad.25.dual_ref), custom_call_target="tpu_custom_call" | custom-call | flops 16777216 | bytes 8519680 | tf_op jit(solution)/shard_map/pallas_call | solution.py:38
  300.0 22.5 %all_to_all.57 = f32[128,1,128]{2,1,0:T(1,128)S(1)} all-to-all(f32[128,1,128]{2,1,0:T(1,128)} %bitcast.73), channel_id=1, replica_groups=mesh['pts'=128,'rep'=2] {'pts'}, dimensions={0} | all-to-all | bytes 131072 | tf_op jit(solution)/shard_map/all_to_all | solution.py:163
  323.1 0.6 select_reduce_fusion.2
  323.7 2.0 collective-permute-start.3
  325.7 0.7 collective-permute-done.3
  326.8 0.6 gather_fusion.7
  327.6 16.5 %all_to_all.58 = f32[128,1,128]{2,1,0:T(1,128)S(1)} all-to-all(f32[128,1,128]{2,1,0:T(1,128)S(1)} %bitcast.84), channel_id=1, replica_groups=mesh['pts'=128,'rep'=2] {'pts'}, dimensions={0} | all-to-all | bytes 131072 | tf_op jit(solution)/shard_map/all_to_all | solution.py:163
  344.2 0.7 pad.26.dual_ref
  344.9 5.4 %shard_map.79 = f32[128,128]{1,0:T(8,128)} custom-call(f32[128,128,128]{2,1,0:T(8,128)} %subtract_multiply_fusion.grid_ref, f32[2,128,128]{2,1,0:T(8,128)} %pad.26.dual_ref), custom_call_target="tpu_custom_call" | custom-call | flops 16777216 | bytes 8519680 | tf_op jit(solution)/shard_map/pallas_call | solution.py:38
  350.3 1.1 select_reduce_fusion.9
  351.4 1.1 select_reduce_fusion.8
  352.6 0.6 gather_fusion.8
  353.3 0.7 pad.27.dual_ref
  354.0 5.4 %shard_map.80 = f32[128,128]{1,0:T(8,128)} custom-call(f32[128,128,128]{2,1,0:T(8,128)} %subtract_multiply_fusion.1.grid_ref.grid_t_ref, f32[2,128,128]{2,1,0:T(8,128)} %pad.27.dual_ref), custom_call_target="tpu_custom_call" | custom-call | flops 16777216 | bytes 8519680 | tf_op jit(solution)/shard_map/pallas_call | solution.py:38
  359.4 17.0 %all_to_all.59 = f32[128,1,128]{2,1,0:T(1,128)S(1)} all-to-all(f32[128,1,128]{2,1,0:T(1,128)} %bitcast.74), channel_id=1, replica_groups=mesh['pts'=128,'rep'=2] {'pts'}, dimensions={0} | all-to-all | bytes 131072 | tf_op jit(solution)/shard_map/all_to_all | solution.py:163
  376.9 0.6 select_reduce_fusion
  377.5 2.6 collective-permute-start.5
  380.2 0.7 collective-permute-done.5
  381.3 0.6 gather_fusion.9
  382.0 16.4 %all_to_all.60 = f32[128,1,128]{2,1,0:T(1,128)S(1)} all-to-all(f32[128,1,128]{2,1,0:T(1,128)S(1)} %bitcast.83), channel_id=1, replica_groups=mesh['pts'=128,'rep'=2] {'pts'}, dimensions={0} | all-to-all | bytes 131072 | tf_op jit(solution)/shard_map/all_to_all | solution.py:163
  398.5 0.7 pad.28.dual_ref
  399.2 5.4 %shard_map.81 = f32[128,128]{1,0:T(8,128)} custom-call(f32[128,128,128]{2,1,0:T(8,128)} %subtract_multiply_fusion.grid_ref, f32[2,128,128]{2,1,0:T(8,128)} %pad.28.dual_ref), custom_call_target="tpu_custom_call" | custom-call | flops 16777216 | bytes 8519680 | tf_op jit(solution)/shard_map/pallas_call | solution.py:38
  404.7 1.1 select_reduce_fusion.7
  405.8 1.1 select_reduce_fusion.6
  406.9 0.6 gather_fusion.10
  407.7 0.7 pad.29.target_ref
  408.4 11.7 %shard_map.82 = f32[12,128,256]{2,1,0:T(8,128)} custom-call(s32[128]{0:T(128)} %copy-done.5, f32[128,128,128]{2,1,0:T(8,128)} %subtract_multiply_fusion.1.grid_ref.grid_t_ref, f32[128,128]{1,0:T(8,128)} %bitcast.64, f32[4,128,128]{2,1,0:T(8,128)} %pad.29.target_ref, bf16[128,128,256]{2,1,0:T(8,128)(2,1)} %all-to-all-done.1.rows_ref, ...), custom_call_target="tpu_custom_call" | custom-call | flops 1090519040 | bytes 19136512 | tf_op jit(solution)/shard_map/pallas_call | solution.py:93
  420.1 1.4 collective-permute-start.7
  421.5 3.3 collective-permute-done.6
  424.8 0.6 fusion.1
  425.4 4.2 maximum_select_fusion
  (52 shorter events, 3.8 us)
Async XLA Ops:
  0.6 21.4 %copy-start.1 = (bf16[3072,256]{1,0:T(8,128)(2,1)S(1)}, bf16[3072,256]{1,0:T(8,128)(2,1)}, u32[]{:S(2)}) copy-start(bf16[3072,256]{1,0:T(8,128)(2,1)} %param.5) | copy-start | bytes 4718596
  5.7 27.3 %all-to-all-start = ((f32[128,2,128]{2,1,0:T(2,128)}), f32[128,2,128]{2,1,0:T(2,128)S(1)}, u32[]{:S(2)}, u32[]{:S(2)}) async-start(f32[128,2,128]{2,1,0:T(2,128)} %copy.43), calls=%async_computation | async-start | bytes 262144 | tf_op jit(solution)/shard_map/all_to_all | solution.py:163
  28.3 14.1 %copy-start.4 = (bf16[3072,256]{1,0:T(8,128)(2,1)S(1)}, bf16[3072,256]{1,0:T(8,128)(2,1)}, u32[]{:S(2)}) copy-start(bf16[3072,256]{1,0:T(8,128)(2,1)} %param.6) | copy-start | bytes 4718596
  33.0 191.6 %all-to-all-start.1 = ((bf16[128,128,256]{2,1,0:T(8,128)(2,1)}), bf16[128,128,256]{2,1,0:T(8,128)(2,1)}, u32[]{:S(2)}, u32[]{:S(2)}) async-start(bf16[128,128,256]{2,1,0:T(8,128)(2,1)} %gather_fusion.3), calls=%async_computation.1 | async-start | bytes 16777216 | tf_op jit(solution)/shard_map/all_to_all | solution.py:163
  42.8 11.8 %copy-start = (bf16[12,128,256]{2,1,0:T(8,128)(2,1)}, bf16[12,128,256]{2,1,0:T(8,128)(2,1)S(1)}, u32[]{:S(2)}) copy-start(bf16[12,128,256]{2,1,0:T(8,128)(2,1)S(1)} %get-tuple-element.8.half_ref) | copy-start | bytes 2359300
  47.5 217.7 %copy-start.5 = (s32[128]{0:T(128)}, s32[128]{0:T(128)S(1)}, u32[]{:S(2)}) copy-start(s32[128]{0:T(128)S(1)} %get-tuple-element.3.keys_ref) | copy-start | bytes 1540
  239.3 21.1 %all-to-all-start.2 = ((f32[128,1,128]{2,1,0:T(1,128)}), f32[128,1,128]{2,1,0:T(1,128)S(1)}, u32[]{:S(2)}, u32[]{:S(2)}) async-start(f32[128,1,128]{2,1,0:T(1,128)} %bitcast.72), calls=%async_computation.2 | async-start | bytes 131072 | tf_op jit(solution)/shard_map/all_to_all | solution.py:163
  261.5 4.8 %collective-permute-start = (f32[24,128]{1,0:T(8,128)S(1)}, f32[24,128]{1,0:T(8,128)S(1)}, u32[]{:S(2)}, u32[]{:S(2)}) collective-permute-start(f32[24,128]{1,0:T(8,128)S(1)} %select_reduce_fusion.5), channel_id=1, source_target_pairs={{0,1},{1,0},{2,3},{3,2},{4,5},{5,4},{6,7},{7,6},{8,9},{9,8},{10,11... | collective-permute-start | bytes 36872 | tf_op jit(solution)/shard_map/ppermute | solution.py:159
  265.1 1.2 collective-permute-start.1
  267.7 17.0 %all-to-all-start.3 = ((f32[128,1,128]{2,1,0:T(1,128)}), f32[128,1,128]{2,1,0:T(1,128)S(1)}, u32[]{:S(2)}, u32[]{:S(2)}) async-start(f32[128,1,128]{2,1,0:T(1,128)} %bitcast.13), calls=%async_computation.3 | async-start | bytes 131072 | tf_op jit(solution)/shard_map/all_to_all | solution.py:163
  323.7 2.8 collective-permute-start.3
  325.6 1.2 collective-permute-start.2
  377.5 3.4 collective-permute-start.5
  380.1 1.2 collective-permute-start.4
  381.3 23.4 %copy-start.2 = (f32[24,128]{1,0:T(8,128)}, f32[24,128]{1,0:T(8,128)S(1)}, u32[]{:S(2)}) copy-start(f32[24,128]{1,0:T(8,128)S(1)} %add_multiply_fusion) | copy-start | bytes 36868
  398.4 6.2 %copy-start.3 = (f32[128,1,128]{2,1,0:T(1,128)}, f32[128,1,128]{2,1,0:T(1,128)S(1)}, u32[]{:S(2)}) copy-start(f32[128,1,128]{2,1,0:T(1,128)S(1)} %all_to_all.60) | copy-start | bytes 196612
  420.1 5.3 %collective-permute-start.7 = (f32[12,128,256]{2,1,0:T(8,128)}, f32[12,128,256]{2,1,0:T(8,128)S(1)}, u32[]{:S(2)}, u32[]{:S(2)}) collective-permute-start(f32[12,128,256]{2,1,0:T(8,128)} %shard_map.82), channel_id=1, source_target_pairs={{0,1},{1,0},{2,3},{3,2},{4,5},{5,4},{6,7},{7,6},{8,9},{9,8},{10,11... | collective-permute-start | bytes 4718600 | tf_op jit(solution)/shard_map/ppermute | solution.py:119
  421.5 3.3 collective-permute-start.6
where the time goes:
time: 436 us; the launch traced here: 430 us
  waiting for transfers between devices  191 us (44%)
  blocking collectives  72.4 us (17%)
  starting transfers between devices  52.5 us (12%)
  Pallas kernels  44.2 us (10%)
  local copies, waits for them, and re-layouts  24.8 us (6%)
  other arithmetic  23.7 us (5%)
  matrix products  18.6 us (4%)
    all_to_all x4, waiting for transfers between devices, a2a(): return lax.all_to_all(value, 'pts', split_axis=0, concat_axis=0, tiled=True)  185 us
    all_to_all x4, blocking collectives, a2a(): return lax.all_to_all(value, 'pts', split_axis=0, concat_axis=0, tiled=True)  72.4 us
    all_to_all x4, starting transfers between devices, a2a(): return lax.all_to_all(value, 'pts', split_axis=0, concat_axis=0, tiled=True)  42.7 us
    pallas_call x6, Pallas kernels, sweep(): pl.pallas_call(sweep_kernel, grid=(pairs // SWEEP_STEP,), in_specs=[pl.Bl...  32.6 us
    pallas_call x1, Pallas kernels, gradient_sums(): pl.pallas_call(gradient_kernel, grid_spec=pltpu.PrefetchScalarGridSpec(nu...  11.7 us
    dot_general x1, matrix products, pair_costs(): jnp.einsum('gjd,gid->gji', target_rows, source_rows, preferred_element_ty...  9.33 us
    dot_general x1, matrix products, pair_costs(): jnp.einsum('gid,gjd->gij', source_rows, target_rows, preferred_element_ty...  9.31 us
  transfers between devices with their start and end apart: 12, of which 10 were waited for; matrix products, arithmetic and copies ran while one was open for 7% of the time, Pallas kernels for 0%

commit v1 on v0

--- a/solution.py
+++ b/solution.py
@@ -27,7 +27,7 @@
     dual_cols = dual_ref[0]
     for p in range(grid_ref.shape[0]):
         dual_col = jnp.broadcast_to(dual_cols[:, p : p + 1], (side, side))
-        scores = (dual_col - grid_ref[p]) * INV_EPS
+        scores = dual_col - grid_ref[p]
         peak = jnp.max(scores, axis=0, keepdims=True)
         mass = jnp.sum(jnp.exp(scores - peak), axis=0, keepdims=True)
         out_ref[p : p + 1, :] = peak + jnp.log(mass)
@@ -53,7 +53,7 @@
 
 
 def gradient_kernel(
-    keys_ref, grid_t_ref, source_ref, target_ref, rows_ref, half_ref, out_ref, mass_ref
+    keys_ref, place_ref, grid_t_ref, source_ref, target_ref, rows_ref, half_ref, out_ref, mass_ref
 ):
     step = pl.program_id(0)
     side = grid_t_ref.shape[1]
@@ -69,7 +69,7 @@
         key = keys_ref[step * GRADIENT_STEP + p]
         slot = jnp.maximum(key, 0)
         target_col = jnp.broadcast_to(target_cols[:, p : p + 1], (side, side))
-        plan_t = jnp.exp((source_ref[p : p + 1, :] + target_col - grid_t_ref[p]) * INV_EPS)
+        plan_t = jnp.exp(source_ref[p : p + 1, :] + target_col - grid_t_ref[p])
         plan_t = jnp.where(key >= 0, plan_t, 0.0)
         weights = plan_t.astype(jnp.bfloat16)
         remainder = (plan_t - weights.astype(jnp.float32)).astype(jnp.bfloat16)
@@ -86,33 +86,33 @@
         out_ref[...] += half_ref[...].astype(jnp.float32) * jnp.concatenate([mass, mass], axis=2)
 
 
-def gradient_sums(keys, grids_t, source_duals, target_duals, rows, half_targets):
+def gradient_sums(keys, place, grids_t, source_duals, target_duals, rows, half_targets):
     pairs, side, _ = grids_t.shape
     width = rows.shape[2]
     half = half_targets.shape[0]
     return pl.pallas_call(
         gradient_kernel,
         grid_spec=pltpu.PrefetchScalarGridSpec(
-            num_scalar_prefetch=1,
+            num_scalar_prefetch=2,
             grid=(pairs // GRADIENT_STEP,),
             in_specs=[
-                pl.BlockSpec((GRADIENT_STEP, side, side), lambda s, k: (s, 0, 0)),
-                pl.BlockSpec((GRADIENT_STEP, side), lambda s, k: (s, 0)),
-                pl.BlockSpec((1, side, side), lambda s, k: (s, 0, 0)),
-                pl.BlockSpec((GRADIENT_STEP, side, width), lambda s, k: (s, 0, 0)),
-                pl.BlockSpec((half, side, width), lambda s, k: (0, 0, 0)),
+                pl.BlockSpec((GRADIENT_STEP, side, side), lambda s, k, w: (s, 0, 0)),
+                pl.BlockSpec((GRADIENT_STEP, side), lambda s, k, w: (s, 0)),
+                pl.BlockSpec((1, side, side), lambda s, k, w: (s, 0, 0)),
+                pl.BlockSpec((GRADIENT_STEP, side, width), lambda s, k, w: (s, 0, 0)),
+                pl.BlockSpec((half, side, width), lambda s, k, w: (0, 0, 0)),
             ],
-            out_specs=pl.BlockSpec((half, side, width), lambda s, k: (0, 0, 0)),
+            out_specs=pl.BlockSpec((half, side, width), lambda s, k, w: (w[0], 0, 0)),
             scratch_shapes=[pltpu.VMEM((half, side, side), jnp.float32)],
         ),
-        out_shape=jax.ShapeDtypeStruct((half, side, width), jnp.float32),
+        out_shape=jax.ShapeDtypeStruct((2 * half, side, width), jnp.float32),
         compiler_params=pltpu.CompilerParams(dimension_semantics=("arbitrary",)),
         cost_estimate=pl.CostEstimate(
             flops=2 * pairs * side * side * width + 8 * pairs * side * side,
             transcendentals=pairs * side * side,
             bytes_accessed=pairs * side * (4 * side + 2 * width) + half * side * width * 6,
         ),
-    )(keys, grids_t, source_duals, columns_of(target_duals, GRADIENT_STEP), rows, half_targets)
+    )(keys, place, grids_t, source_duals, columns_of(target_duals, GRADIENT_STEP), rows, half_targets)
 
 
 def both_halves(mine, rep_index):
@@ -135,9 +135,9 @@
     inner_dot_t = jnp.einsum(
         "gjd,gid->gji", target_rows, source_rows, preferred_element_type=jnp.float32
     )
-    width = source_rows.shape[2]
-    grid = (source_sq[:, :, None] + target_sq[:, None, :] - 2.0 * inner_dot) / width
-    grid_t = (source_sq[:, None, :] + target_sq[:, :, None] - 2.0 * inner_dot_t) / width
+    scale = INV_EPS / source_rows.shape[2]
+    grid = (source_sq[:, :, None] + target_sq[:, None, :] - 2.0 * inner_dot) * scale
+    grid_t = (source_sq[:, None, :] + target_sq[:, :, None] - 2.0 * inner_dot_t) * scale
     return grid, grid_t
 
 
@@ -217,19 +217,25 @@
         merged_totals = totals * jnp.exp(maxima - merged) + other_totals * jnp.exp(
             other_maxima - merged
         )
-        source_dual = -EPSILON * (merged + jnp.log(merged_totals))
-        sent_duals = jnp.where(served[:, None], source_dual[source_index], 0.0)
+        source_lse = merged + jnp.log(merged_totals)
+        source_dual = -EPSILON * source_lse
+        sent_duals = jnp.where(served[:, None], -source_lse[source_index], 0.0)
         source_here = a2a(sent_duals)
         column_lse = sweep(cost_grid, source_here)
         col_max, col_tot = combine_by(column_lse, half_key, half_blocks)
-        target_half = -EPSILON * (col_max + jnp.log(col_tot))
+        target_lse = col_max + jnp.log(col_tot)
+        target_half = -target_lse
 
     target_here = target_half[half_pick]
-    gradient_half = gradient_sums(
-        half_key, cost_grid_t, source_here, target_here, received, own_half
-    )
-    target_dual = both_halves(target_half, rep_index)
-    gradient = both_halves(gradient_half, rep_index)
+    gradient_mine = gradient_sums(
+        half_key, rep_index.reshape(1), cost_grid_t, source_here, target_here, received, own_half
+    )
+    gradient_half = lax.dynamic_slice_in_dim(gradient_mine, lower_block, half_blocks, 0)
+    target_dual = both_halves(-EPSILON * target_lse, rep_index)
+    gradient_other = lax.ppermute(gradient_half, "rep", [(0, 1), (1, 0)])
+    gradient = lax.dynamic_update_slice_in_dim(
+        gradient_mine, gradient_other, (1 - rep_index) * half_blocks, 0
+    )
     return (
         source_dual.reshape(-1),
         target_dual.reshape(-1),

time: 436 us -> 438 us (level)
  local copies, waits for them, and re-layouts: 24.8 us -> 31.1 us
where the time goes in v1:
time: 438 us; the launch traced here: 432 us
  waiting for transfers between devices  191 us (44%)
  blocking collectives  72.5 us (17%)
  starting transfers between devices  52.8 us (12%)
  Pallas kernels  43.7 us (10%)
  local copies, waits for them, and re-layouts  31.1 us (7%)
  other arithmetic  20.1 us (5%)
  matrix products  18.7 us (4%)
    all_to_all x4, waiting for transfers between devices, a2a(): return lax.all_to_all(value, 'pts', split_axis=0, concat_axis=0, tiled=True)  184 us
    all_to_all x4, blocking collectives, a2a(): return lax.all_to_all(value, 'pts', split_axis=0, concat_axis=0, tiled=True)  72.5 us
    all_to_all x4, starting transfers between devices, a2a(): return lax.all_to_all(value, 'pts', split_axis=0, concat_axis=0, tiled=True)  42.9 us
    pallas_call x6, Pallas kernels, sweep(): pl.pallas_call(sweep_kernel, grid=(pairs // SWEEP_STEP,), in_specs=[pl.Bl...  32.6 us
    pallas_call x1, Pallas kernels, gradient_sums(): pl.pallas_call(gradient_kernel, grid_spec=pltpu.PrefetchScalarGridSpec(nu...  11 us
    dot_general x1, matrix products, pair_costs(): jnp.einsum('gid,gjd->gij', source_rows, target_rows, preferred_element_ty...  9.35 us
    dot_general x1, matrix products, pair_costs(): jnp.einsum('gjd,gid->gji', target_rows, source_rows, preferred_element_ty...  9.31 us
  transfers between devices with their start and end apart: 12, of which 10 were waited for; matrix products, arithmetic and copies ran while one was open for 7% of the time, Pallas kernels for 0%

profile of v1, /device:TPU:1, one launch (start us, length us, event | category | flops | bytes accessed | tf_op | source)
XLA Modules:
  0.0 431.8 jit_solution(715361694448368338)
XLA Ops:
  1.4 0.7 fusion.10
  2.3 1.9 multiply_reduce_fusion
  4.2 0.6 gather_fusion
  4.9 0.8 copy.43
  5.7 16.3 %all-to-all-start = ((f32[128,2,128]{2,1,0:T(2,128)}), f32[128,2,128]{2,1,0:T(2,128)S(1)}, u32[]{:S(2)}, u32[]{:S(2)}) async-start(f32[128,2,128]{2,1,0:T(2,128)} %copy.43), calls=%async_computation | async-start | bytes 262144 | tf_op jit(solution)/shard_map/all_to_all | solution.py:163
  22.0 6.5 %gather_fusion.3 = bf16[128,128,256]{2,1,0:T(8,128)(2,1)} fusion(bf16[24,128,256]{2,1,0:T(8,128)(2,1)S(1)} %bitcast.58, s32[1024]{0:T(1024)S(1)} %pad_clamp_fusion.1), kind=kCustom, calls=%fused_computation.3 | custom fusion | bytes 16777728 | tf_op jit(solution)/shard_map/gather | solution.py:188
  28.5 4.5 %all-to-all-done = f32[128,2,128]{2,1,0:T(2,128)S(1)} async-done(((f32[128,2,128]{2,1,0:T(2,128)}), f32[128,2,128]{2,1,0:T(2,128)S(1)}, u32[]{:S(2)}, u32[]{:S(2)}) %all-to-all-start) | async-done | bytes 131104 | tf_op jit(solution)/shard_map/all_to_all | solution.py:163
  33.0 9.6 %all-to-all-start.1 = ((bf16[128,128,256]{2,1,0:T(8,128)(2,1)}), bf16[128,128,256]{2,1,0:T(8,128)(2,1)}, u32[]{:S(2)}, u32[]{:S(2)}) async-start(bf16[128,128,256]{2,1,0:T(8,128)(2,1)} %gather_fusion.3), calls=%async_computation.1 | async-start | bytes 16777216 | tf_op jit(solution)/shard_map/all_to_all | solution.py:163
  42.9 4.7 %fusion.13 = (s32[128]{0:T(128)S(1)}, s32[128]{0:T(128)S(1)}) fusion(s32[]{:T(128)S(6)} %mul.48, f32[128,2,128]{2,1,0:T(2,128)S(1)} %all-to-all-done), kind=kLoop, calls=%fused_computation.76 | loop fusion | flops 640 | bytes 1540 | tf_op jit(solution)/shard_map/jit(_where)/select_n | solution.py:202
  47.6 0.6 gather_fusion.1
  48.3 6.4 %gather_fusion.2 = bf16[128,128,256]{2,1,0:T(8,128)(2,1)} fusion(bf16[12,128,256]{2,1,0:T(8,128)(2,1)S(1)} %get-tuple-element.10.half_ref, s32[1024]{0:T(1024)S(1)} %pad_clamp_fusion), kind=kCustom, calls=%fused_computation.2 | custom fusion | bytes 16777728 | tf_op jit(solution)/shard_map/gather | solution.py:205
  54.7 0.6 gather_fusion.4
  55.4 0.7 pad.23.dual_ref
  56.2 168.3 %all-to-all-done.1.rows_ref = bf16[128,128,256]{2,1,0:T(8,128)(2,1)} async-done(((bf16[128,128,256]{2,1,0:T(8,128)(2,1)}), bf16[128,128,256]{2,1,0:T(8,128)(2,1)}, u32[]{:S(2)}, u32[]{:S(2)}) %all-to-all-start.1) | async-done | bytes 8388640 | tf_op jit(solution)/shard_map/all_to_all | solution.py:163
  224.4 9.3 %subtract_multiply_fusion.1.grid_ref.grid_t_ref = f32[128,128,128]{2,1,0:T(8,128)} fusion(f32[128,128]{1,0:T(8,128)S(1)} %gather_fusion.1, f32[128,128]{1,0:T(8,128)S(1)} %bitcast.61, bf16[128,128,256]{2,1,0:T(8,128)(2,1)} %gather_fusion.2, bf16[128,128,256]{2,1,0:T(8,128)(2,1)} %all-to-all-done.1.rows_ref), kind=kOutput, calls=%fused_computation.12 | convolution fusion | flops 1082130432 | bytes 25296896 | tf_op jit(solution)/shard_map/gjd,gid->gji/dot_general | solution.py:135
  233.8 5.4 %shard_map.76 = f32[128,128]{1,0:T(8,128)} custom-call(f32[128,128,128]{2,1,0:T(8,128)} %subtract_multiply_fusion.1.grid_ref.grid_t_ref, f32[2,128,128]{2,1,0:T(8,128)} %pad.23.dual_ref), custom_call_target="tpu_custom_call" | custom-call | flops 16777216 | bytes 8519680 | tf_op jit(solution)/shard_map/pallas_call | solution.py:38
  239.2 10.7 %all-to-all-start.2 = ((f32[128,1,128]{2,1,0:T(1,128)}), f32[128,1,128]{2,1,0:T(1,128)S(1)}, u32[]{:S(2)}, u32[]{:S(2)}) async-start(f32[128,1,128]{2,1,0:T(1,128)} %bitcast.73), calls=%async_computation.2 | async-start | bytes 131072 | tf_op jit(solution)/shard_map/all_to_all | solution.py:163
  249.9 10.6 %all-to-all-done.2 = f32[128,1,128]{2,1,0:T(1,128)S(1)} async-done(((f32[128,1,128]{2,1,0:T(1,128)}), f32[128,1,128]{2,1,0:T(1,128)S(1)}, u32[]{:S(2)}, u32[]{:S(2)}) %all-to-all-start.2) | async-done | bytes 65568 | tf_op jit(solution)/shard_map/all_to_all | solution.py:163
  261.6 3.6 collective-permute-start
  265.3 1.1 collective-permute-done.1
  266.4 0.6 gather_fusion.5
  267.0 0.7 bitcast_select_fusion.2
  267.7 6.4 %all-to-all-start.3 = ((f32[128,1,128]{2,1,0:T(1,128)}), f32[128,1,128]{2,1,0:T(1,128)S(1)}, u32[]{:S(2)}, u32[]{:S(2)}) async-start(f32[128,1,128]{2,1,0:T(1,128)} %bitcast.13), calls=%async_computation.3 | async-start | bytes 131072 | tf_op jit(solution)/shard_map/all_to_all | solution.py:163
  274.1 9.3 %subtract_multiply_fusion.grid_ref = f32[128,128,128]{2,1,0:T(8,128)} fusion(f32[128,128]{1,0:T(8,128)S(1)} %gather_fusion.1, f32[128,128]{1,0:T(8,128)S(1)} %bitcast.62, bf16[128,128,256]{2,1,0:T(8,128)(2,1)} %all-to-all-done.1.rows_ref, bf16[128,128,256]{2,1,0:T(8,128)(2,1)} %gather_fusion.2), kind=kOutput, calls=%fused_computation.11 | convolution fusion | flops 1082130432 | bytes 25296896 | tf_op jit(solution)/shard_map/gid,gjd->gij/dot_general | solution.py:132
  283.5 1.2 all-to-all-done.3
  284.8 0.7 pad.24.dual_ref
  285.4 5.4 %shard_map.77 = f32[128,128]{1,0:T(8,128)} custom-call(f32[128,128,128]{2,1,0:T(8,128)} %subtract_multiply_fusion.grid_ref, f32[2,128,128]{2,1,0:T(8,128)} %pad.24.dual_ref), custom_call_target="tpu_custom_call" | custom-call | flops 16777216 | bytes 8519680 | tf_op jit(solution)/shard_map/pallas_call | solution.py:38
  290.9 1.1 select_reduce_fusion.11
  292.0 1.1 select_reduce_fusion.10
  293.1 0.6 gather_fusion.6
  293.9 0.7 pad.25.dual_ref
  294.6 5.4 %shard_map.78 = f32[128,128]{1,0:T(8,128)} custom-call(f32[128,128,128]{2,1,0:T(8,128)} %subtract_multiply_fusion.1.grid_ref.grid_t_ref, f32[2,128,128]{2,1,0:T(8,128)} %pad.25.dual_ref), custom_call_target="tpu_custom_call" | custom-call | flops 16777216 | bytes 8519680 | tf_op jit(solution)/shard_map/pallas_call | solution.py:38
  300.0 22.6 %all_to_all.57 = f32[128,1,128]{2,1,0:T(1,128)S(1)} all-to-all(f32[128,1,128]{2,1,0:T(1,128)} %bitcast.74), channel_id=1, replica_groups=mesh['pts'=128,'rep'=2] {'pts'}, dimensions={0} | all-to-all | bytes 131072 | tf_op jit(solution)/shard_map/all_to_all | solution.py:163
  323.8 2.0 collective-permute-start.3
  325.9 0.7 collective-permute-done.3
  327.0 0.6 gather_fusion.7
  327.7 16.5 %all_to_all.58 = f32[128,1,128]{2,1,0:T(1,128)S(1)} all-to-all(f32[128,1,128]{2,1,0:T(1,128)S(1)} %bitcast.85), channel_id=1, replica_groups=mesh['pts'=128,'rep'=2] {'pts'}, dimensions={0} | all-to-all | bytes 131072 | tf_op jit(solution)/shard_map/all_to_all | solution.py:163
  344.3 0.7 pad.26.dual_ref
  345.0 5.4 %shard_map.79 = f32[128,128]{1,0:T(8,128)} custom-call(f32[128,128,128]{2,1,0:T(8,128)} %subtract_multiply_fusion.grid_ref, f32[2,128,128]{2,1,0:T(8,128)} %pad.26.dual_ref), custom_call_target="tpu_custom_call" | custom-call | flops 16777216 | bytes 8519680 | tf_op jit(solution)/shard_map/pallas_call | solution.py:38
  350.4 1.1 select_reduce_fusion.9
  351.6 1.1 select_reduce_fusion.8
  352.7 0.6 gather_fusion.8
  353.5 0.7 pad.27.dual_ref
  354.1 5.4 %shard_map.80 = f32[128,128]{1,0:T(8,128)} custom-call(f32[128,128,128]{2,1,0:T(8,128)} %subtract_multiply_fusion.1.grid_ref.grid_t_ref, f32[2,128,128]{2,1,0:T(8,128)} %pad.27.dual_ref), custom_call_target="tpu_custom_call" | custom-call | flops 16777216 | bytes 8519680 | tf_op jit(solution)/shard_map/pallas_call | solution.py:38
  359.6 16.9 %all_to_all.59 = f32[128,1,128]{2,1,0:T(1,128)S(1)} all-to-all(f32[128,1,128]{2,1,0:T(1,128)} %bitcast.75), channel_id=1, replica_groups=mesh['pts'=128,'rep'=2] {'pts'}, dimensions={0} | all-to-all | bytes 131072 | tf_op jit(solution)/shard_map/all_to_all | solution.py:163
  377.0 0.6 select_reduce_fusion
  377.6 2.6 collective-permute-start.5
  380.3 0.7 collective-permute-done.5
  381.4 0.6 multiply_bitcast_fusion
  382.0 0.6 gather_fusion.9
  382.8 16.4 %all_to_all.60 = f32[128,1,128]{2,1,0:T(1,128)S(1)} all-to-all(f32[128,1,128]{2,1,0:T(1,128)S(1)} %bitcast.84), channel_id=1, replica_groups=mesh['pts'=128,'rep'=2] {'pts'}, dimensions={0} | all-to-all | bytes 131072 | tf_op jit(solution)/shard_map/all_to_all | solution.py:163
  399.3 0.7 pad.28.dual_ref
  400.0 5.4 %shard_map.81 = f32[128,128]{1,0:T(8,128)} custom-call(f32[128,128,128]{2,1,0:T(8,128)} %subtract_multiply_fusion.grid_ref, f32[2,128,128]{2,1,0:T(8,128)} %pad.28.dual_ref), custom_call_target="tpu_custom_call" | custom-call | flops 16777216 | bytes 8519680 | tf_op jit(solution)/shard_map/pallas_call | solution.py:38
  405.4 1.1 select_reduce_fusion.7
  406.5 1.1 select_reduce_fusion.6
  407.7 0.6 gather_fusion.10
  408.5 0.7 pad.29.target_ref
  409.2 11.0 %shard_map.82 = f32[24,128,256]{2,1,0:T(8,128)} custom-call(s32[128]{0:T(128)} %copy-done.6, s32[1]{0:T(128)} %bitcast.36.place_ref, f32[128,128,128]{2,1,0:T(8,128)} %subtract_multiply_fusion.1.grid_ref.grid_t_ref, f32[128,128]{1,0:T(8,128)} %bitcast.65, f32[4,128,128]{2,1,0:T(8,128)} %pad.29.target_ref, bf16[128,128,256]{2,1,0:T(8,128)(2,1)} %all-to-all-done.1.rows_ref, ...), custom_call_target="tpu_custom_call" | custom-call | flops 1090519040 | bytes 19136512 | tf_op jit(solution)/shard_map/pallas_call | solution.py:93
  420.2 2.8 constant_dynamic-slice_fusion
  423.0 1.3 collective-permute-start.7
  424.4 3.4 collective-permute-done.6
  427.8 0.6 fusion.1
  428.4 1.6 constant_dynamic-update-slice_fusion
  430.0 1.7 copy-done.3
  (55 shorter events, 5.5 us)
Async XLA Ops:
  0.6 21.4 %copy-start.1 = (bf16[3072,256]{1,0:T(8,128)(2,1)S(1)}, bf16[3072,256]{1,0:T(8,128)(2,1)}, u32[]{:S(2)}) copy-start(bf16[3072,256]{1,0:T(8,128)(2,1)} %param.5) | copy-start | bytes 4718596
  5.7 27.3 %all-to-all-start = ((f32[128,2,128]{2,1,0:T(2,128)}), f32[128,2,128]{2,1,0:T(2,128)S(1)}, u32[]{:S(2)}, u32[]{:S(2)}) async-start(f32[128,2,128]{2,1,0:T(2,128)} %copy.43), calls=%async_computation | async-start | bytes 262144 | tf_op jit(solution)/shard_map/all_to_all | solution.py:163
  28.5 14.0 %copy-start.5 = (bf16[3072,256]{1,0:T(8,128)(2,1)S(1)}, bf16[3072,256]{1,0:T(8,128)(2,1)}, u32[]{:S(2)}) copy-start(bf16[3072,256]{1,0:T(8,128)(2,1)} %param.6) | copy-start | bytes 4718596
  33.0 191.5 %all-to-all-start.1 = ((bf16[128,128,256]{2,1,0:T(8,128)(2,1)}), bf16[128,128,256]{2,1,0:T(8,128)(2,1)}, u32[]{:S(2)}, u32[]{:S(2)}) async-start(bf16[128,128,256]{2,1,0:T(8,128)(2,1)} %gather_fusion.3), calls=%async_computation.1 | async-start | bytes 16777216 | tf_op jit(solution)/shard_map/all_to_all | solution.py:163
  42.8 11.9 %copy-start = (bf16[12,128,256]{2,1,0:T(8,128)(2,1)}, bf16[12,128,256]{2,1,0:T(8,128)(2,1)S(1)}, u32[]{:S(2)}) copy-start(bf16[12,128,256]{2,1,0:T(8,128)(2,1)S(1)} %get-tuple-element.10.half_ref) | copy-start | bytes 2359300
  47.6 217.7 %copy-start.6 = (s32[128]{0:T(128)}, s32[128]{0:T(128)S(1)}, u32[]{:S(2)}) copy-start(s32[128]{0:T(128)S(1)} %get-tuple-element.3.keys_ref) | copy-start | bytes 1540
  239.2 21.3 %all-to-all-start.2 = ((f32[128,1,128]{2,1,0:T(1,128)}), f32[128,1,128]{2,1,0:T(1,128)S(1)}, u32[]{:S(2)}, u32[]{:S(2)}) async-start(f32[128,1,128]{2,1,0:T(1,128)} %bitcast.73), calls=%async_computation.2 | async-start | bytes 131072 | tf_op jit(solution)/shard_map/all_to_all | solution.py:163
  261.6 4.8 %collective-permute-start = (f32[24,128]{1,0:T(8,128)S(1)}, f32[24,128]{1,0:T(8,128)S(1)}, u32[]{:S(2)}, u32[]{:S(2)}) collective-permute-start(f32[24,128]{1,0:T(8,128)S(1)} %select_reduce_fusion.5), channel_id=1, source_target_pairs={{0,1},{1,0},{2,3},{3,2},{4,5},{5,4},{6,7},{7,6},{8,9},{9,8},{10,11... | collective-permute-start | bytes 36872 | tf_op jit(solution)/shard_map/ppermute | solution.py:159
  265.2 1.2 collective-permute-start.1
  267.7 16.9 %all-to-all-start.3 = ((f32[128,1,128]{2,1,0:T(1,128)}), f32[128,1,128]{2,1,0:T(1,128)S(1)}, u32[]{:S(2)}, u32[]{:S(2)}) async-start(f32[128,1,128]{2,1,0:T(1,128)} %bitcast.13), calls=%async_computation.3 | async-start | bytes 131072 | tf_op jit(solution)/shard_map/all_to_all | solution.py:163
  323.8 2.8 collective-permute-start.3
  325.8 1.2 collective-permute-start.2
  377.6 3.5 collective-permute-start.5
  380.2 1.2 collective-permute-start.4
  399.2 6.2 %copy-start.4 = (f32[128,1,128]{2,1,0:T(1,128)}, f32[128,1,128]{2,1,0:T(1,128)S(1)}, u32[]{:S(2)}) copy-start(f32[128,1,128]{2,1,0:T(1,128)S(1)} %all_to_all.60) | copy-start | bytes 196612
  420.2 8.2 %copy-start.2 = (f32[24,128,256]{2,1,0:T(8,128)S(1)}, f32[24,128,256]{2,1,0:T(8,128)}, u32[]{:S(2)}) copy-start(f32[24,128,256]{2,1,0:T(8,128)} %shard_map.82) | copy-start | bytes 9437188
  423.0 5.3 %collective-permute-start.7 = (f32[12,128,256]{2,1,0:T(8,128)}, f32[12,128,256]{2,1,0:T(8,128)}, u32[]{:S(2)}, u32[]{:S(2)}) collective-permute-start(f32[12,128,256]{2,1,0:T(8,128)} %constant_dynamic-slice_fusion), channel_id=1, source_target_pairs={{0,1},{1,0},{2,3},{3,2},{4,5},{5,4},{6,7},{7,6},{8,9},{9,8},{10,11... | collective-permute-start | bytes 4718600 | tf_op jit(solution)/shard_map/ppermute | solution.py:235
  424.4 3.4 collective-permute-start.6
  430.0 1.7 copy-start.3

commit v2 on v0

--- a/solution.py
+++ b/solution.py
@@ -13,7 +13,7 @@
 NEG_BIG = -1e30
 INV_EPS = 1.0 / EPSILON
 SWEEP_STEP = 64
-GRADIENT_STEP = 32
+GRADIENT_STEP = 64
 
 
 def columns_of(duals, step):

time: 436 us -> 436 us (level)
  no operation moved by 1% of the time
where the time goes in v2:
time: 436 us; the launch traced here: 430 us
  waiting for transfers between devices  191 us (44%)
  blocking collectives  72.4 us (17%)
  starting transfers between devices  53.1 us (12%)
  Pallas kernels  44.4 us (10%)
  local copies, waits for them, and re-layouts  24.8 us (6%)
  other arithmetic  23.7 us (5%)
  matrix products  18.6 us (4%)
    all_to_all x4, waiting for transfers between devices, a2a(): return lax.all_to_all(value, 'pts', split_axis=0, concat_axis=0, tiled=True)  184 us
    all_to_all x4, blocking collectives, a2a(): return lax.all_to_all(value, 'pts', split_axis=0, concat_axis=0, tiled=True)  72.4 us
    all_to_all x4, starting transfers between devices, a2a(): return lax.all_to_all(value, 'pts', split_axis=0, concat_axis=0, tiled=True)  43.5 us
    pallas_call x6, Pallas kernels, sweep(): pl.pallas_call(sweep_kernel, grid=(pairs // SWEEP_STEP,), in_specs=[pl.Bl...  32.6 us
    pallas_call x1, Pallas kernels, gradient_sums(): pl.pallas_call(gradient_kernel, grid_spec=pltpu.PrefetchScalarGridSpec(nu...  11.9 us
    dot_general x1, matrix products, pair_costs(): jnp.einsum('gid,gjd->gij', source_rows, target_rows, preferred_element_ty...  9.32 us
    dot_general x1, matrix products, pair_costs(): jnp.einsum('gjd,gid->gji', target_rows, source_rows, preferred_element_ty...  9.31 us
  transfers between devices with their start and end apart: 12, of which 10 were waited for; matrix products, arithmetic and copies ran while one was open for 7% of the time, Pallas kernels for 0%

profile of v2, /device:TPU:1, one launch (start us, length us, event | category | flops | bytes accessed | tf_op | source)
XLA Modules:
  0.0 429.9 jit_solution(2067597754833427981)
XLA Ops:
  1.4 0.7 fusion.9
  2.3 1.9 multiply_reduce_fusion
  4.2 0.6 gather_fusion
  4.9 0.8 copy.43
  5.7 16.3 %all-to-all-start = ((f32[128,2,128]{2,1,0:T(2,128)}), f32[128,2,128]{2,1,0:T(2,128)S(1)}, u32[]{:S(2)}, u32[]{:S(2)}) async-start(f32[128,2,128]{2,1,0:T(2,128)} %copy.43), calls=%async_computation | async-start | bytes 262144 | tf_op jit(solution)/shard_map/all_to_all | solution.py:163
  22.0 6.4 %gather_fusion.3 = bf16[128,128,256]{2,1,0:T(8,128)(2,1)} fusion(bf16[24,128,256]{2,1,0:T(8,128)(2,1)S(1)} %bitcast.56, s32[1024]{0:T(1024)S(1)} %pad_clamp_fusion.1), kind=kCustom, calls=%fused_computation.3 | custom fusion | bytes 16777728 | tf_op jit(solution)/shard_map/gather | solution.py:188
  28.4 4.5 %all-to-all-done = f32[128,2,128]{2,1,0:T(2,128)S(1)} async-done(((f32[128,2,128]{2,1,0:T(2,128)}), f32[128,2,128]{2,1,0:T(2,128)S(1)}, u32[]{:S(2)}, u32[]{:S(2)}) %all-to-all-start) | async-done | bytes 131104 | tf_op jit(solution)/shard_map/all_to_all | solution.py:163
  33.0 9.6 %all-to-all-start.1 = ((bf16[128,128,256]{2,1,0:T(8,128)(2,1)}), bf16[128,128,256]{2,1,0:T(8,128)(2,1)}, u32[]{:S(2)}, u32[]{:S(2)}) async-start(bf16[128,128,256]{2,1,0:T(8,128)(2,1)} %gather_fusion.3), calls=%async_computation.1 | async-start | bytes 16777216 | tf_op jit(solution)/shard_map/all_to_all | solution.py:163
  43.0 4.7 %fusion.12 = (s32[128]{0:T(128)S(1)}, s32[128]{0:T(128)S(1)}) fusion(s32[]{:T(128)S(6)} %mul.45, f32[128,2,128]{2,1,0:T(2,128)S(1)} %all-to-all-done), kind=kLoop, calls=%fused_computation.72 | loop fusion | flops 640 | bytes 1540 | tf_op jit(solution)/shard_map/jit(_where)/select_n | solution.py:202
  47.7 0.6 gather_fusion.1
  48.3 6.4 %gather_fusion.2 = bf16[128,128,256]{2,1,0:T(8,128)(2,1)} fusion(bf16[12,128,256]{2,1,0:T(8,128)(2,1)S(1)} %get-tuple-element.8.half_ref, s32[1024]{0:T(1024)S(1)} %pad_clamp_fusion), kind=kCustom, calls=%fused_computation.2 | custom fusion | bytes 16777728 | tf_op jit(solution)/shard_map/gather | solution.py:205
  54.7 0.6 gather_fusion.4
  55.5 0.7 pad.22.dual_ref
  56.2 167.9 %all-to-all-done.1.rows_ref = bf16[128,128,256]{2,1,0:T(8,128)(2,1)} async-done(((bf16[128,128,256]{2,1,0:T(8,128)(2,1)}), bf16[128,128,256]{2,1,0:T(8,128)(2,1)}, u32[]{:S(2)}, u32[]{:S(2)}) %all-to-all-start.1) | async-done | bytes 8388640 | tf_op jit(solution)/shard_map/all_to_all | solution.py:163
  224.1 9.3 %subtract_multiply_fusion.1.grid_ref.grid_t_ref = f32[128,128,128]{2,1,0:T(8,128)} fusion(f32[128,128]{1,0:T(8,128)S(1)} %gather_fusion.1, f32[128,128]{1,0:T(8,128)S(1)} %bitcast.60, bf16[128,128,256]{2,1,0:T(8,128)(2,1)} %gather_fusion.2, bf16[128,128,256]{2,1,0:T(8,128)(2,1)} %all-to-all-done.1.rows_ref), kind=kOutput, calls=%fused_computation.12 | convolution fusion | flops 1082130432 | bytes 25296896 | tf_op jit(solution)/shard_map/gjd,gid->gji/dot_general | solution.py:135
  233.4 5.4 %shard_map.76 = f32[128,128]{1,0:T(8,128)} custom-call(f32[128,128,128]{2,1,0:T(8,128)} %subtract_multiply_fusion.1.grid_ref.grid_t_ref, f32[2,128,128]{2,1,0:T(8,128)} %pad.22.dual_ref), custom_call_target="tpu_custom_call" | custom-call | flops 16777216 | bytes 8519680 | tf_op jit(solution)/shard_map/pallas_call | solution.py:38
  238.9 11.2 %all-to-all-start.2 = ((f32[128,1,128]{2,1,0:T(1,128)}), f32[128,1,128]{2,1,0:T(1,128)S(1)}, u32[]{:S(2)}, u32[]{:S(2)}) async-start(f32[128,1,128]{2,1,0:T(1,128)} %bitcast.72), calls=%async_computation.2 | async-start | bytes 131072 | tf_op jit(solution)/shard_map/all_to_all | solution.py:163
  250.1 10.6 %all-to-all-done.2 = f32[128,1,128]{2,1,0:T(1,128)S(1)} async-done(((f32[128,1,128]{2,1,0:T(1,128)}), f32[128,1,128]{2,1,0:T(1,128)S(1)}, u32[]{:S(2)}, u32[]{:S(2)}) %all-to-all-start.2) | async-done | bytes 65568 | tf_op jit(solution)/shard_map/all_to_all | solution.py:163
  260.7 0.6 select_reduce_fusion.5
  261.2 0.6 select_reduce_fusion.4
  261.8 3.4 collective-permute-start
  265.3 1.1 collective-permute-done.1
  266.4 0.6 gather_fusion.5
  267.1 0.7 bitcast_select_fusion.2
  267.8 6.4 %all-to-all-start.3 = ((f32[128,1,128]{2,1,0:T(1,128)}), f32[128,1,128]{2,1,0:T(1,128)S(1)}, u32[]{:S(2)}, u32[]{:S(2)}) async-start(f32[128,1,128]{2,1,0:T(1,128)} %bitcast.13), calls=%async_computation.3 | async-start | bytes 131072 | tf_op jit(solution)/shard_map/all_to_all | solution.py:163
  274.1 9.3 %subtract_multiply_fusion.grid_ref = f32[128,128,128]{2,1,0:T(8,128)} fusion(f32[128,128]{1,0:T(8,128)S(1)} %gather_fusion.1, f32[128,128]{1,0:T(8,128)S(1)} %bitcast.61, bf16[128,128,256]{2,1,0:T(8,128)(2,1)} %all-to-all-done.1.rows_ref, bf16[128,128,256]{2,1,0:T(8,128)(2,1)} %gather_fusion.2), kind=kOutput, calls=%fused_computation.11 | convolution fusion | flops 1082130432 | bytes 25296896 | tf_op jit(solution)/shard_map/gid,gjd->gij/dot_general | solution.py:132
  283.5 1.3 all-to-all-done.3
  284.9 0.7 pad.23.dual_ref
  285.5 5.4 %shard_map.77 = f32[128,128]{1,0:T(8,128)} custom-call(f32[128,128,128]{2,1,0:T(8,128)} %subtract_multiply_fusion.grid_ref, f32[2,128,128]{2,1,0:T(8,128)} %pad.23.dual_ref), custom_call_target="tpu_custom_call" | custom-call | flops 16777216 | bytes 8519680 | tf_op jit(solution)/shard_map/pallas_call | solution.py:38
  290.9 1.1 select_reduce_fusion.11
  292.1 1.1 select_reduce_fusion.10
  293.2 0.6 gather_fusion.6
  294.0 0.7 pad.24.dual_ref
  294.6 5.4 %shard_map.78 = f32[128,128]{1,0:T(8,128)} custom-call(f32[128,128,128]{2,1,0:T(8,128)} %subtract_multiply_fusion.1.grid_ref.grid_t_ref, f32[2,128,128]{2,1,0:T(8,128)} %pad.24.dual_ref), custom_call_target="tpu_custom_call" | custom-call | flops 16777216 | bytes 8519680 | tf_op jit(solution)/shard_map/pallas_call | solution.py:38
  300.1 22.5 %all_to_all.57 = f32[128,1,128]{2,1,0:T(1,128)S(1)} all-to-all(f32[128,1,128]{2,1,0:T(1,128)} %bitcast.73), channel_id=1, replica_groups=mesh['pts'=128,'rep'=2] {'pts'}, dimensions={0} | all-to-all | bytes 131072 | tf_op jit(solution)/shard_map/all_to_all | solution.py:163
  323.2 0.6 select_reduce_fusion.2
  323.8 2.0 collective-permute-start.3
  325.8 0.7 collective-permute-done.3
  326.9 0.6 gather_fusion.7
  327.7 16.5 %all_to_all.58 = f32[128,1,128]{2,1,0:T(1,128)S(1)} all-to-all(f32[128,1,128]{2,1,0:T(1,128)S(1)} %bitcast.84), channel_id=1, replica_groups=mesh['pts'=128,'rep'=2] {'pts'}, dimensions={0} | all-to-all | bytes 131072 | tf_op jit(solution)/shard_map/all_to_all | solution.py:163
  344.3 0.7 pad.25.dual_ref
  345.0 5.4 %shard_map.79 = f32[128,128]{1,0:T(8,128)} custom-call(f32[128,128,128]{2,1,0:T(8,128)} %subtract_multiply_fusion.grid_ref, f32[2,128,128]{2,1,0:T(8,128)} %pad.25.dual_ref), custom_call_target="tpu_custom_call" | custom-call | flops 16777216 | bytes 8519680 | tf_op jit(solution)/shard_map/pallas_call | solution.py:38
  350.4 1.1 select_reduce_fusion.9
  351.5 1.1 select_reduce_fusion.8
  352.7 0.6 gather_fusion.8
  353.4 0.7 pad.26.dual_ref
  354.1 5.4 %shard_map.80 = f32[128,128]{1,0:T(8,128)} custom-call(f32[128,128,128]{2,1,0:T(8,128)} %subtract_multiply_fusion.1.grid_ref.grid_t_ref, f32[2,128,128]{2,1,0:T(8,128)} %pad.26.dual_ref), custom_call_target="tpu_custom_call" | custom-call | flops 16777216 | bytes 8519680 | tf_op jit(solution)/shard_map/pallas_call | solution.py:38
  359.5 17.0 %all_to_all.59 = f32[128,1,128]{2,1,0:T(1,128)S(1)} all-to-all(f32[128,1,128]{2,1,0:T(1,128)} %bitcast.74), channel_id=1, replica_groups=mesh['pts'=128,'rep'=2] {'pts'}, dimensions={0} | all-to-all | bytes 131072 | tf_op jit(solution)/shard_map/all_to_all | solution.py:163
  377.0 0.6 select_reduce_fusion
  377.6 2.6 collective-permute-start.5
  380.3 0.7 collective-permute-done.5
  381.4 0.6 gather_fusion.9
  382.1 16.4 %all_to_all.60 = f32[128,1,128]{2,1,0:T(1,128)S(1)} all-to-all(f32[128,1,128]{2,1,0:T(1,128)S(1)} %bitcast.83), channel_id=1, replica_groups=mesh['pts'=128,'rep'=2] {'pts'}, dimensions={0} | all-to-all | bytes 131072 | tf_op jit(solution)/shard_map/all_to_all | solution.py:163
  398.6 0.7 pad.27.dual_ref
  399.3 5.4 %shard_map.81 = f32[128,128]{1,0:T(8,128)} custom-call(f32[128,128,128]{2,1,0:T(8,128)} %subtract_multiply_fusion.grid_ref, f32[2,128,128]{2,1,0:T(8,128)} %pad.27.dual_ref), custom_call_target="tpu_custom_call" | custom-call | flops 16777216 | bytes 8519680 | tf_op jit(solution)/shard_map/pallas_call | solution.py:38
  404.8 1.1 select_reduce_fusion.7
  405.9 1.1 select_reduce_fusion.6
  407.0 0.6 gather_fusion.10
  407.8 0.7 pad.28.target_ref
  408.4 11.9 %shard_map.82 = f32[12,128,256]{2,1,0:T(8,128)} custom-call(s32[128]{0:T(128)} %copy-done.5, f32[128,128,128]{2,1,0:T(8,128)} %subtract_multiply_fusion.1.grid_ref.grid_t_ref, f32[128,128]{1,0:T(8,128)} %bitcast.63, f32[2,128,128]{2,1,0:T(8,128)} %pad.28.target_ref, bf16[128,128,256]{2,1,0:T(8,128)(2,1)} %all-to-all-done.1.rows_ref, ...), custom_call_target="tpu_custom_call" | custom-call | flops 1090519040 | bytes 19136512 | tf_op jit(solution)/shard_map/pallas_call | solution.py:93
  420.3 1.4 collective-permute-start.7
  421.7 3.3 collective-permute-done.6
  425.0 0.6 fusion.1
  425.6 4.2 maximum_select_fusion
  (52 shorter events, 3.7 us)
Async XLA Ops:
  0.6 21.4 %copy-start.1 = (bf16[3072,256]{1,0:T(8,128)(2,1)S(1)}, bf16[3072,256]{1,0:T(8,128)(2,1)}, u32[]{:S(2)}) copy-start(bf16[3072,256]{1,0:T(8,128)(2,1)} %param.5) | copy-start | bytes 4718596
  5.7 27.3 %all-to-all-start = ((f32[128,2,128]{2,1,0:T(2,128)}), f32[128,2,128]{2,1,0:T(2,128)S(1)}, u32[]{:S(2)}, u32[]{:S(2)}) async-start(f32[128,2,128]{2,1,0:T(2,128)} %copy.43), calls=%async_computation | async-start | bytes 262144 | tf_op jit(solution)/shard_map/all_to_all | solution.py:163
  28.4 14.2 %copy-start.4 = (bf16[3072,256]{1,0:T(8,128)(2,1)S(1)}, bf16[3072,256]{1,0:T(8,128)(2,1)}, u32[]{:S(2)}) copy-start(bf16[3072,256]{1,0:T(8,128)(2,1)} %param.6) | copy-start | bytes 4718596
  33.0 191.2 %all-to-all-start.1 = ((bf16[128,128,256]{2,1,0:T(8,128)(2,1)}), bf16[128,128,256]{2,1,0:T(8,128)(2,1)}, u32[]{:S(2)}, u32[]{:S(2)}) async-start(bf16[128,128,256]{2,1,0:T(8,128)(2,1)} %gather_fusion.3), calls=%async_computation.1 | async-start | bytes 16777216 | tf_op jit(solution)/shard_map/all_to_all | solution.py:163
  42.9 11.9 %copy-start = (bf16[12,128,256]{2,1,0:T(8,128)(2,1)}, bf16[12,128,256]{2,1,0:T(8,128)(2,1)S(1)}, u32[]{:S(2)}) copy-start(bf16[12,128,256]{2,1,0:T(8,128)(2,1)S(1)} %get-tuple-element.8.half_ref) | copy-start | bytes 2359300
  47.6 217.7 %copy-start.5 = (s32[128]{0:T(128)}, s32[128]{0:T(128)S(1)}, u32[]{:S(2)}) copy-start(s32[128]{0:T(128)S(1)} %get-tuple-element.3.keys_ref) | copy-start | bytes 1540
  238.9 21.8 %all-to-all-start.2 = ((f32[128,1,128]{2,1,0:T(1,128)}), f32[128,1,128]{2,1,0:T(1,128)S(1)}, u32[]{:S(2)}, u32[]{:S(2)}) async-start(f32[128,1,128]{2,1,0:T(1,128)} %bitcast.72), calls=%async_computation.2 | async-start | bytes 131072 | tf_op jit(solution)/shard_map/all_to_all | solution.py:163
  261.8 4.6 %collective-permute-start = (f32[24,128]{1,0:T(8,128)S(1)}, f32[24,128]{1,0:T(8,128)S(1)}, u32[]{:S(2)}, u32[]{:S(2)}) collective-permute-start(f32[24,128]{1,0:T(8,128)S(1)} %select_reduce_fusion.5), channel_id=1, source_target_pairs={{0,1},{1,0},{2,3},{3,2},{4,5},{5,4},{6,7},{7,6},{8,9},{9,8},{10,11... | collective-permute-start | bytes 36872 | tf_op jit(solution)/shard_map/ppermute | solution.py:159
  265.2 1.2 collective-permute-start.1
  267.8 17.0 %all-to-all-start.3 = ((f32[128,1,128]{2,1,0:T(1,128)}), f32[128,1,128]{2,1,0:T(1,128)S(1)}, u32[]{:S(2)}, u32[]{:S(2)}) async-start(f32[128,1,128]{2,1,0:T(1,128)} %bitcast.13), calls=%async_computation.3 | async-start | bytes 131072 | tf_op jit(solution)/shard_map/all_to_all | solution.py:163
  323.8 2.8 collective-permute-start.3
  325.7 1.2 collective-permute-start.2
  377.6 3.4 collective-permute-start.5
  380.2 1.2 collective-permute-start.4
  381.4 23.4 %copy-start.2 = (f32[24,128]{1,0:T(8,128)}, f32[24,128]{1,0:T(8,128)S(1)}, u32[]{:S(2)}) copy-start(f32[24,128]{1,0:T(8,128)S(1)} %add_multiply_fusion) | copy-start | bytes 36868
  398.5 6.2 %copy-start.3 = (f32[128,1,128]{2,1,0:T(1,128)}, f32[128,1,128]{2,1,0:T(1,128)S(1)}, u32[]{:S(2)}) copy-start(f32[128,1,128]{2,1,0:T(1,128)S(1)} %all_to_all.60) | copy-start | bytes 196612
  420.3 5.3 %collective-permute-start.7 = (f32[12,128,256]{2,1,0:T(8,128)}, f32[12,128,256]{2,1,0:T(8,128)S(1)}, u32[]{:S(2)}, u32[]{:S(2)}) collective-permute-start(f32[12,128,256]{2,1,0:T(8,128)} %shard_map.82), channel_id=1, source_target_pairs={{0,1},{1,0},{2,3},{3,2},{4,5},{5,4},{6,7},{7,6},{8,9},{9,8},{10,11... | collective-permute-start | bytes 4718600 | tf_op jit(solution)/shard_map/ppermute | solution.py:119
  421.7 3.3 collective-permute-start.6

commit v3 on v2

--- a/solution.py
+++ b/solution.py
@@ -12,7 +12,7 @@
 EPSILON = 0.05
 NEG_BIG = -1e30
 INV_EPS = 1.0 / EPSILON
-SWEEP_STEP = 64
+SWEEP_STEP = 128
 GRADIENT_STEP = 64
 
 

time: 436 us -> 442 us (1.014)
  Pallas kernels: 44.4 us -> 50.8 us
    pallas_call x6, Pallas kernels: 32.6 us -> 38.9 us  [sweep(): pl.pallas_call(sweep_kernel, grid=(pairs // SWEEP_STEP,), in_specs=[pl.Bl...]
where the time goes in v3:
time: 442 us; the launch traced here: 436 us
  waiting for transfers between devices  191 us (43%)
  blocking collectives  72 us (16%)
  starting transfers between devices  53.2 us (12%)
  Pallas kernels  50.8 us (11%)
  local copies, waits for them, and re-layouts  24.7 us (6%)
  other arithmetic  23.7 us (5%)
  matrix products  18.7 us (4%)
    all_to_all x4, waiting for transfers between devices, a2a(): return lax.all_to_all(value, 'pts', split_axis=0, concat_axis=0, tiled=True)  185 us
    all_to_all x4, blocking collectives, a2a(): return lax.all_to_all(value, 'pts', split_axis=0, concat_axis=0, tiled=True)  72 us
    all_to_all x4, starting transfers between devices, a2a(): return lax.all_to_all(value, 'pts', split_axis=0, concat_axis=0, tiled=True)  42.8 us
    pallas_call x6, Pallas kernels, sweep(): pl.pallas_call(sweep_kernel, grid=(pairs // SWEEP_STEP,), in_specs=[pl.Bl...  38.9 us
    pallas_call x1, Pallas kernels, gradient_sums(): pl.pallas_call(gradient_kernel, grid_spec=pltpu.PrefetchScalarGridSpec(nu...  11.9 us
    dot_general x1, matrix products, pair_costs(): jnp.einsum('gid,gjd->gij', source_rows, target_rows, preferred_element_ty...  9.34 us
    dot_general x1, matrix products, pair_costs(): jnp.einsum('gjd,gid->gji', target_rows, source_rows, preferred_element_ty...  9.31 us
    ppermute x6, starting transfers between devices, swap_rep(): return lax.ppermute(value, 'rep', [(0, 1), (1, 0)])  9.02 us
  transfers between devices with their start and end apart: 12, of which 10 were waited for; matrix products, arithmetic and copies ran while one was open for 7% of the time, Pallas kernels for 0%

profile of v3, /device:TPU:1, one launch (start us, length us, event | category | flops | bytes accessed | tf_op | source)
XLA Modules:
  0.0 436.2 jit_solution(3913160293147498905)
XLA Ops:
  1.4 0.7 fusion.9
  2.3 1.9 multiply_reduce_fusion
  4.2 0.6 gather_fusion
  4.9 0.8 copy.35
  5.7 16.3 %all-to-all-start = ((f32[128,2,128]{2,1,0:T(2,128)}), f32[128,2,128]{2,1,0:T(2,128)S(1)}, u32[]{:S(2)}, u32[]{:S(2)}) async-start(f32[128,2,128]{2,1,0:T(2,128)} %copy.35), calls=%async_computation | async-start | bytes 262144 | tf_op jit(solution)/shard_map/all_to_all | solution.py:163
  22.0 6.4 %gather_fusion.3 = bf16[128,128,256]{2,1,0:T(8,128)(2,1)} fusion(bf16[24,128,256]{2,1,0:T(8,128)(2,1)S(1)} %bitcast.62, s32[1024]{0:T(1024)S(1)} %pad_clamp_fusion.1), kind=kCustom, calls=%fused_computation.3 | custom fusion | bytes 16777728 | tf_op jit(solution)/shard_map/gather | solution.py:188
  28.4 4.5 %all-to-all-done = f32[128,2,128]{2,1,0:T(2,128)S(1)} async-done(((f32[128,2,128]{2,1,0:T(2,128)}), f32[128,2,128]{2,1,0:T(2,128)S(1)}, u32[]{:S(2)}, u32[]{:S(2)}) %all-to-all-start) | async-done | bytes 131104 | tf_op jit(solution)/shard_map/all_to_all | solution.py:163
  33.0 9.6 %all-to-all-start.1 = ((bf16[128,128,256]{2,1,0:T(8,128)(2,1)}), bf16[128,128,256]{2,1,0:T(8,128)(2,1)}, u32[]{:S(2)}, u32[]{:S(2)}) async-start(bf16[128,128,256]{2,1,0:T(8,128)(2,1)} %gather_fusion.3), calls=%async_computation.1 | async-start | bytes 16777216 | tf_op jit(solution)/shard_map/all_to_all | solution.py:163
  42.9 4.7 %fusion.12 = (s32[128]{0:T(128)S(1)}, s32[128]{0:T(128)S(1)}) fusion(s32[]{:T(128)S(6)} %mul.45, f32[128,2,128]{2,1,0:T(2,128)S(1)} %all-to-all-done), kind=kLoop, calls=%fused_computation.72 | loop fusion | flops 640 | bytes 1540 | tf_op jit(solution)/shard_map/jit(_where)/select_n | solution.py:202
  47.6 0.6 gather_fusion.1
  48.3 6.4 %gather_fusion.2 = bf16[128,128,256]{2,1,0:T(8,128)(2,1)} fusion(bf16[12,128,256]{2,1,0:T(8,128)(2,1)S(1)} %get-tuple-element.8.half_ref, s32[1024]{0:T(1024)S(1)} %pad_clamp_fusion), kind=kCustom, calls=%fused_computation.2 | custom fusion | bytes 16777728 | tf_op jit(solution)/shard_map/gather | solution.py:205
  54.7 0.6 gather_fusion.4
  55.4 0.7 copy.36
  56.1 168.3 %all-to-all-done.1.rows_ref = bf16[128,128,256]{2,1,0:T(8,128)(2,1)} async-done(((bf16[128,128,256]{2,1,0:T(8,128)(2,1)}), bf16[128,128,256]{2,1,0:T(8,128)(2,1)}, u32[]{:S(2)}, u32[]{:S(2)}) %all-to-all-start.1) | async-done | bytes 8388640 | tf_op jit(solution)/shard_map/all_to_all | solution.py:163
  224.4 9.3 %subtract_multiply_fusion.1.grid_ref.grid_t_ref = f32[128,128,128]{2,1,0:T(8,128)} fusion(f32[128,128]{1,0:T(8,128)S(1)} %gather_fusion.1, f32[128,128]{1,0:T(8,128)S(1)} %bitcast.66, bf16[128,128,256]{2,1,0:T(8,128)(2,1)} %gather_fusion.2, bf16[128,128,256]{2,1,0:T(8,128)(2,1)} %all-to-all-done.1.rows_ref), kind=kOutput, calls=%fused_computation.12 | convolution fusion | flops 1082130432 | bytes 25296896 | tf_op jit(solution)/shard_map/gjd,gid->gji/dot_general | solution.py:135
  233.7 6.5 %shard_map.76 = f32[128,128]{1,0:T(8,128)} custom-call(f32[128,128,128]{2,1,0:T(8,128)} %subtract_multiply_fusion.1.grid_ref.grid_t_ref, f32[1,128,128]{2,1,0:T(8,128)} %bitcast.71), custom_call_target="tpu_custom_call" | custom-call | flops 16777216 | bytes 8519680 | tf_op jit(solution)/shard_map/pallas_call | solution.py:38
  240.2 10.7 %all-to-all-start.2 = ((f32[128,1,128]{2,1,0:T(1,128)}), f32[128,1,128]{2,1,0:T(1,128)S(1)}, u32[]{:S(2)}, u32[]{:S(2)}) async-start(f32[128,1,128]{2,1,0:T(1,128)} %bitcast.72), calls=%async_computation.2 | async-start | bytes 131072 | tf_op jit(solution)/shard_map/all_to_all | solution.py:163
  251.0 10.6 %all-to-all-done.2 = f32[128,1,128]{2,1,0:T(1,128)S(1)} async-done(((f32[128,1,128]{2,1,0:T(1,128)}), f32[128,1,128]{2,1,0:T(1,128)S(1)}, u32[]{:S(2)}, u32[]{:S(2)}) %all-to-all-start.2) | async-done | bytes 65568 | tf_op jit(solution)/shard_map/all_to_all | solution.py:163
  261.6 0.6 select_reduce_fusion.5
  262.1 0.6 select_reduce_fusion.4
  262.7 3.9 collective-permute-start
  266.8 1.1 collective-permute-done.1
  267.9 0.6 gather_fusion.5
  268.5 0.7 bitcast_select_fusion.2
  269.2 6.2 %all-to-all-start.3 = ((f32[128,1,128]{2,1,0:T(1,128)}), f32[128,1,128]{2,1,0:T(1,128)S(1)}, u32[]{:S(2)}, u32[]{:S(2)}) async-start(f32[128,1,128]{2,1,0:T(1,128)} %bitcast.13), calls=%async_computation.3 | async-start | bytes 131072 | tf_op jit(solution)/shard_map/all_to_all | solution.py:163
  275.4 9.3 %subtract_multiply_fusion.grid_ref = f32[128,128,128]{2,1,0:T(8,128)} fusion(f32[128,128]{1,0:T(8,128)S(1)} %gather_fusion.1, f32[128,128]{1,0:T(8,128)S(1)} %bitcast.67, bf16[128,128,256]{2,1,0:T(8,128)(2,1)} %all-to-all-done.1.rows_ref, bf16[128,128,256]{2,1,0:T(8,128)(2,1)} %gather_fusion.2), kind=kOutput, calls=%fused_computation.11 | convolution fusion | flops 1082130432 | bytes 25296896 | tf_op jit(solution)/shard_map/gid,gjd->gij/dot_general | solution.py:132
  284.7 1.3 all-to-all-done.3
  286.0 0.7 copy.39
  286.7 6.5 %shard_map.77 = f32[128,128]{1,0:T(8,128)} custom-call(f32[128,128,128]{2,1,0:T(8,128)} %subtract_multiply_fusion.grid_ref, f32[1,128,128]{2,1,0:T(8,128)} %bitcast.73), custom_call_target="tpu_custom_call" | custom-call | flops 16777216 | bytes 8519680 | tf_op jit(solution)/shard_map/pallas_call | solution.py:38
  293.2 1.1 select_reduce_fusion.11
  294.3 1.1 select_reduce_fusion.10
  295.5 0.6 gather_fusion.6
  296.1 0.7 copy.40
  296.9 6.5 %shard_map.78 = f32[128,128]{1,0:T(8,128)} custom-call(f32[128,128,128]{2,1,0:T(8,128)} %subtract_multiply_fusion.1.grid_ref.grid_t_ref, f32[1,128,128]{2,1,0:T(8,128)} %bitcast.74), custom_call_target="tpu_custom_call" | custom-call | flops 16777216 | bytes 8519680 | tf_op jit(solution)/shard_map/pallas_call | solution.py:38
  303.3 22.8 %all_to_all.57 = f32[128,1,128]{2,1,0:T(1,128)S(1)} all-to-all(f32[128,1,128]{2,1,0:T(1,128)} %bitcast.75), channel_id=1, replica_groups=mesh['pts'=128,'rep'=2] {'pts'}, dimensions={0} | all-to-all | bytes 131072 | tf_op jit(solution)/shard_map/all_to_all | solution.py:163
  326.7 0.6 select_reduce_fusion.2
  327.3 2.0 collective-permute-start.3
  329.4 0.7 collective-permute-done.3
  330.5 0.6 gather_fusion.7
  331.2 16.1 %all_to_all.58 = f32[128,1,128]{2,1,0:T(1,128)S(1)} all-to-all(f32[128,1,128]{2,1,0:T(1,128)S(1)} %bitcast.87), channel_id=1, replica_groups=mesh['pts'=128,'rep'=2] {'pts'}, dimensions={0} | all-to-all | bytes 131072 | tf_op jit(solution)/shard_map/all_to_all | solution.py:163
  347.3 0.7 copy.43
  348.1 6.5 %shard_map.79 = f32[128,128]{1,0:T(8,128)} custom-call(f32[128,128,128]{2,1,0:T(8,128)} %subtract_multiply_fusion.grid_ref, f32[1,128,128]{2,1,0:T(8,128)} %bitcast.76), custom_call_target="tpu_custom_call" | custom-call | flops 16777216 | bytes 8519680 | tf_op jit(solution)/shard_map/pallas_call | solution.py:38
  354.6 1.1 select_reduce_fusion.9
  355.7 1.1 select_reduce_fusion.8
  356.8 0.6 gather_fusion.8
  357.5 0.7 copy.44
  358.2 6.5 %shard_map.80 = f32[128,128]{1,0:T(8,128)} custom-call(f32[128,128,128]{2,1,0:T(8,128)} %subtract_multiply_fusion.1.grid_ref.grid_t_ref, f32[1,128,128]{2,1,0:T(8,128)} %bitcast.77), custom_call_target="tpu_custom_call" | custom-call | flops 16777216 | bytes 8519680 | tf_op jit(solution)/shard_map/pallas_call | solution.py:38
  364.7 17.0 %all_to_all.59 = f32[128,1,128]{2,1,0:T(1,128)S(1)} all-to-all(f32[128,1,128]{2,1,0:T(1,128)} %bitcast.78), channel_id=1, replica_groups=mesh['pts'=128,'rep'=2] {'pts'}, dimensions={0} | all-to-all | bytes 131072 | tf_op jit(solution)/shard_map/all_to_all | solution.py:163
  382.2 0.6 select_reduce_fusion
  382.8 2.8 collective-permute-start.5
  385.8 0.7 collective-permute-done.5
  386.9 0.6 gather_fusion.9
  387.6 16.1 %all_to_all.60 = f32[128,1,128]{2,1,0:T(1,128)S(1)} all-to-all(f32[128,1,128]{2,1,0:T(1,128)S(1)} %bitcast.86), channel_id=1, replica_groups=mesh['pts'=128,'rep'=2] {'pts'}, dimensions={0} | all-to-all | bytes 131072 | tf_op jit(solution)/shard_map/all_to_all | solution.py:163
  403.7 0.7 copy.47
  404.4 6.5 %shard_map.81 = f32[128,128]{1,0:T(8,128)} custom-call(f32[128,128,128]{2,1,0:T(8,128)} %subtract_multiply_fusion.grid_ref, f32[1,128,128]{2,1,0:T(8,128)} %bitcast.79), custom_call_target="tpu_custom_call" | custom-call | flops 16777216 | bytes 8519680 | tf_op jit(solution)/shard_map/pallas_call | solution.py:38
  410.9 1.1 select_reduce_fusion.7
  412.1 1.1 select_reduce_fusion.6
  413.2 0.6 gather_fusion.10
  414.0 0.7 pad.4.target_ref
  414.6 11.9 %shard_map.82 = f32[12,128,256]{2,1,0:T(8,128)} custom-call(s32[128]{0:T(128)} %copy-done.5, f32[128,128,128]{2,1,0:T(8,128)} %subtract_multiply_fusion.1.grid_ref.grid_t_ref, f32[128,128]{1,0:T(8,128)} %bitcast.68, f32[2,128,128]{2,1,0:T(8,128)} %pad.4.target_ref, bf16[128,128,256]{2,1,0:T(8,128)(2,1)} %all-to-all-done.1.rows_ref, bf16[12,128,256]{2,1,0:T(8,128)(2,1)} %copy-done), custom_call_target="tpu_custom_call" | custom-call | flops 1090519040 | bytes 19136512 | tf_op jit(solution)/shard_map/pallas_call | solution.py:93
  426.5 1.4 collective-permute-start.7
  427.9 3.3 collective-permute-done.6
  431.2 0.6 fusion.1
  431.8 4.2 maximum_select_fusion
  (46 shorter events, 3.2 us)
Async XLA Ops:
  0.6 21.4 %copy-start.1 = (bf16[3072,256]{1,0:T(8,128)(2,1)S(1)}, bf16[3072,256]{1,0:T(8,128)(2,1)}, u32[]{:S(2)}) copy-start(bf16[3072,256]{1,0:T(8,128)(2,1)} %param.5) | copy-start | bytes 4718596
  5.7 27.3 %all-to-all-start = ((f32[128,2,128]{2,1,0:T(2,128)}), f32[128,2,128]{2,1,0:T(2,128)S(1)}, u32[]{:S(2)}, u32[]{:S(2)}) async-start(f32[128,2,128]{2,1,0:T(2,128)} %copy.35), calls=%async_computation | async-start | bytes 262144 | tf_op jit(solution)/shard_map/all_to_all | solution.py:163
  28.4 14.1 %copy-start.4 = (bf16[3072,256]{1,0:T(8,128)(2,1)S(1)}, bf16[3072,256]{1,0:T(8,128)(2,1)}, u32[]{:S(2)}) copy-start(bf16[3072,256]{1,0:T(8,128)(2,1)} %param.6) | copy-start | bytes 4718596
  33.0 191.5 %all-to-all-start.1 = ((bf16[128,128,256]{2,1,0:T(8,128)(2,1)}), bf16[128,128,256]{2,1,0:T(8,128)(2,1)}, u32[]{:S(2)}, u32[]{:S(2)}) async-start(bf16[128,128,256]{2,1,0:T(8,128)(2,1)} %gather_fusion.3), calls=%async_computation.1 | async-start | bytes 16777216 | tf_op jit(solution)/shard_map/all_to_all | solution.py:163
  42.8 11.9 %copy-start = (bf16[12,128,256]{2,1,0:T(8,128)(2,1)}, bf16[12,128,256]{2,1,0:T(8,128)(2,1)S(1)}, u32[]{:S(2)}) copy-start(bf16[12,128,256]{2,1,0:T(8,128)(2,1)S(1)} %get-tuple-element.8.half_ref) | copy-start | bytes 2359300
  47.6 219.2 %copy-start.5 = (s32[128]{0:T(128)}, s32[128]{0:T(128)S(1)}, u32[]{:S(2)}) copy-start(s32[128]{0:T(128)S(1)} %get-tuple-element.3.keys_ref) | copy-start | bytes 1540
  240.2 21.3 %all-to-all-start.2 = ((f32[128,1,128]{2,1,0:T(1,128)}), f32[128,1,128]{2,1,0:T(1,128)S(1)}, u32[]{:S(2)}, u32[]{:S(2)}) async-start(f32[128,1,128]{2,1,0:T(1,128)} %bitcast.72), calls=%async_computation.2 | async-start | bytes 131072 | tf_op jit(solution)/shard_map/all_to_all | solution.py:163
  262.7 5.1 %collective-permute-start = (f32[24,128]{1,0:T(8,128)S(1)}, f32[24,128]{1,0:T(8,128)S(1)}, u32[]{:S(2)}, u32[]{:S(2)}) collective-permute-start(f32[24,128]{1,0:T(8,128)S(1)} %select_reduce_fusion.5), channel_id=1, source_target_pairs={{0,1},{1,0},{2,3},{3,2},{4,5},{5,4},{6,7},{7,6},{8,9},{9,8},{10,11... | collective-permute-start | bytes 36872 | tf_op jit(solution)/shard_map/ppermute | solution.py:159
  266.7 1.2 collective-permute-start.1
  269.2 16.8 %all-to-all-start.3 = ((f32[128,1,128]{2,1,0:T(1,128)}), f32[128,1,128]{2,1,0:T(1,128)S(1)}, u32[]{:S(2)}, u32[]{:S(2)}) async-start(f32[128,1,128]{2,1,0:T(1,128)} %bitcast.13), calls=%async_computation.3 | async-start | bytes 131072 | tf_op jit(solution)/shard_map/all_to_all | solution.py:163
  327.3 2.8 collective-permute-start.3
  329.3 1.2 collective-permute-start.2
  382.8 3.7 collective-permute-start.5
  385.7 1.2 collective-permute-start.4
  386.9 24.1 %copy-start.2 = (f32[24,128]{1,0:T(8,128)}, f32[24,128]{1,0:T(8,128)S(1)}, u32[]{:S(2)}) copy-start(f32[24,128]{1,0:T(8,128)S(1)} %add_multiply_fusion) | copy-start | bytes 36868
  403.7 7.2 %copy-start.3 = (f32[128,1,128]{2,1,0:T(1,128)}, f32[128,1,128]{2,1,0:T(1,128)S(1)}, u32[]{:S(2)}) copy-start(f32[128,1,128]{2,1,0:T(1,128)S(1)} %all_to_all.60) | copy-start | bytes 196612
  426.5 5.3 %collective-permute-start.7 = (f32[12,128,256]{2,1,0:T(8,128)}, f32[12,128,256]{2,1,0:T(8,128)S(1)}, u32[]{:S(2)}, u32[]{:S(2)}) collective-permute-start(f32[12,128,256]{2,1,0:T(8,128)} %shard_map.82), channel_id=1, source_target_pairs={{0,1},{1,0},{2,3},{3,2},{4,5},{5,4},{6,7},{7,6},{8,9},{9,8},{10,11... | collective-permute-start | bytes 4718600 | tf_op jit(solution)/shard_map/ppermute | solution.py:119
  427.9 3.3 collective-permute-start.6
